TPU v7x, 512 devices: a whole 4x8x8 slice. The times are simulated.
512 devices in a mesh: replica: 8 (over x, core), shard: 8 (over z), tensor: 8 (over y).
Axes of the slice: x: 4, y: 8, z: 8, core: 2. Of those that a mesh axis runs over, the one named last changes fastest.
Arguments:
- inproj_grads: bfloat16 [8, 1536, 3328], P('replica', 'shard', 'tensor'), may hold values from -6 to 6
- inproj_error: float32 [8, 1536, 3328], P('replica', 'shard', 'tensor'), may hold values from -6 to 6
- inproj_weight: float32 [1536, 3328], P('shard', 'tensor'), may hold values from -6 to 6
- inproj_moment: float32 [1536, 3328], P('shard', 'tensor'), may hold values from -6 to 6
- inproj_query: float32 [3328, 32], P('tensor'), may hold values from -0.109375 to 0.109375
- outproj_grads: bfloat16 [8, 3072, 1536], P('replica', 'shard', 'tensor'), may hold values from -6 to 6
- outproj_error: float32 [8, 3072, 1536], P('replica', 'shard', 'tensor'), may hold values from -6 to 6
- outproj_weight: float32 [3072, 1536], P('shard', 'tensor'), may hold values from -6 to 6
- outproj_moment: float32 [3072, 1536], P('shard', 'tensor'), may hold values from -6 to 6
- outproj_query: float32 [1536, 32], P('tensor'), may hold values from -0.15625 to 0.15625
Outputs:
- inproj_master: float32 [1536, 3328], P('shard', 'tensor')
- inproj_velocity: float32 [1536, 3328], P('shard', 'tensor')
- inproj_residue: float32 [8, 1536, 3328], P('replica', 'shard', 'tensor')
- inproj_basis: float32 [3328, 32], P('tensor')
- outproj_master: float32 [3072, 1536], P('shard', 'tensor')
- outproj_velocity: float32 [3072, 1536], P('shard', 'tensor')
- outproj_residue: float32 [8, 3072, 1536], P('replica', 'shard', 'tensor')
- outproj_basis: float32 [1536, 32], P('tensor')
All inputs are finite; a program needn't handle non-finite values.
Results may differ from a plain program's by a relative error of at most 0.0003.
Values sent between devices are 32-bit elements; how exact they have to be, the bound alone decides.
No kernel may reach another device: no remote copies, remote signals or barrier semaphores. Data moves between devices by JAX's collectives and lax.ppermute only.
A program may use at most 64 MiB of HBM per device.

v0:
```python
import jax
import jax.numpy as jnp
from jax import lax
from jax.sharding import PartitionSpec as P

ROUNDS = 2
NS_STEPS = 4


MOMENTUM_DECAY = 0.9
LEARN_RATE = 0.1
EPSILON = 1e-06


def precise_dot(left, right):
    return jnp.dot(left, right, precision=lax.Precision.HIGHEST, preferred_element_type=jnp.float32)


def inverse_root(gram_sum):
    identity = jnp.eye(gram_sum.shape[0], dtype=jnp.float32)
    norm_scale = jnp.sqrt(jnp.sum(gram_sum * gram_sum) + EPSILON)
    current = gram_sum / norm_scale
    inverse = identity
    for sweep in range(NS_STEPS):
        middle = 0.5 * (3.0 * identity - precise_dot(inverse, current))
        current = precise_dot(current, middle)
        inverse = precise_dot(middle, inverse)
    return inverse / jnp.sqrt(norm_scale)


def finish(merged, orthonormal, query, weight, moment):
    approx = precise_dot(orthonormal, query.T)
    residue = (merged - approx)[None]
    velocity = MOMENTUM_DECAY * moment + approx
    master = weight - LEARN_RATE * velocity
    return (master, velocity, residue, query)


def per_device(
    inproj_grads,
    inproj_error,
    inproj_weight,
    inproj_moment,
    inproj_query,
    outproj_grads,
    outproj_error,
    outproj_weight,
    outproj_moment,
    outproj_query,
):
    replicas = lax.axis_size("replica")
    merged_in = inproj_grads[0].astype(jnp.float32) + inproj_error[0]
    merged_out = outproj_grads[0].astype(jnp.float32) + outproj_error[0]
    query_in = inproj_query
    query_out = outproj_query
    for power_round in range(ROUNDS):
        partial_in = precise_dot(merged_in, query_in)
        partial_out = precise_dot(merged_out, query_out)
        summed_in, summed_out = lax.psum((partial_in, partial_out), ("replica", "tensor"))
        projected_in = summed_in / replicas
        projected_out = summed_out / replicas
        gram_in, gram_out = lax.psum(
            (
                precise_dot(projected_in.T, projected_in),
                precise_dot(projected_out.T, projected_out),
            ),
            "shard",
        )
        ortho_in = precise_dot(projected_in, inverse_root(gram_in))
        ortho_out = precise_dot(projected_out, inverse_root(gram_out))
        column_in = jnp.einsum(
            "nm,nk->mk",
            merged_in,
            ortho_in,
            precision=lax.Precision.HIGHEST,
            preferred_element_type=jnp.float32,
        )
        column_out = jnp.einsum(
            "nm,nk->mk",
            merged_out,
            ortho_out,
            precision=lax.Precision.HIGHEST,
            preferred_element_type=jnp.float32,
        )
        summed_cin, summed_cout = lax.psum((column_in, column_out), ("replica", "shard"))
        query_in = summed_cin / replicas
        query_out = summed_cout / replicas
    first = finish(merged_in, ortho_in, query_in, inproj_weight, inproj_moment)
    second = finish(merged_out, ortho_out, query_out, outproj_weight, outproj_moment)
    return (first[0], first[1], first[2], first[3], second[0], second[1], second[2], second[3])


def solution(mesh):
    return jax.shard_map(
        per_device,
        mesh=mesh,
        in_specs=(
            P("replica", "shard", "tensor"),
            P("replica", "shard", "tensor"),
            P("shard", "tensor"),
            P("shard", "tensor"),
            P("tensor", None),
            P("replica", "shard", "tensor"),
            P("replica", "shard", "tensor"),
            P("shard", "tensor"),
            P("shard", "tensor"),
            P("tensor", None),
        ),
        out_specs=(
            P("shard", "tensor"),
            P("shard", "tensor"),
            P("replica", "shard", "tensor"),
            P("tensor", None),
            P("shard", "tensor"),
            P("shard", "tensor"),
            P("replica", "shard", "tensor"),
            P("tensor", None),
        ),
        check_vma=False,
    )
```

profile of v0, /device:TPU:1, one launch (start us, length us, event | category | flops | bytes accessed | tf_op | source)
XLA Modules:
  0.0 834.6 jit_solution(8912133169515081752)
XLA Ops:
  7.3 0.8 copy-done
  8.0 2.1 fusion.22
  10.1 1.0 fusion.31
  11.2 189.4 %all-reduce.13.cloned.1.call-done = (f32[192,32]{0,1:T(8,128)}, f32[384,32]{0,1:T(8,128)}) async-done(((f32[192,32]{0,1:T(8,128)}, f32[384,32]{0,1:T(8,128)}), (f32[192,32]{0,1:T(8,128)}, f32[384,32]{0,1:T(8,128)})) %all-reduce.13.cloned.1.call-update) | async-done | bytes 73744 | tf_op jit(solution)/shard_map/psum | solution.py:59
  200.6 1.0 fusion.51
  201.6 0.2 fusion.41
  201.8 23.8 %all-reduce.5 = (f32[32,32]{1,0:T(8,128)S(1)}, f32[32,32]{1,0:T(8,128)S(1)}) all-reduce(f32[32,32]{1,0:T(8,128)S(1)} %fusion.51, f32[32,32]{1,0:T(8,128)S(1)} %fusion.41), channel_id=1, replica_groups=mesh['replica'=8,'shard'=8,'tensor'=8] {'shard'}, use_global_device_ids=true, to_apply=%region_1.0 | all-reduce | flops 2048 | bytes 16384 | tf_op jit(solution)/shard_map/psum | solution.py:62
  225.6 0.6 multiply_reduce_fusion.1
  227.4 0.2 fusion.6
  227.7 0.1 fusion.88
  227.8 0.2 fusion.5
  229.5 0.2 fusion.14
  230.2 0.1 fusion.83
  230.4 0.2 fusion.12
  230.6 0.1 convolution_divide_fusion.3
  230.7 0.3 fusion.49
  231.1 1.0 fusion.20
  232.3 0.1 convolution_divide_fusion.1
  232.4 0.5 fusion.39
  232.9 1.1 fusion.29
  234.1 185.1 %all-reduce.17.cloned.1.call-done = (f32[416,32]{0,1:T(8,128)}, f32[192,32]{0,1:T(8,128)}) async-done(((f32[416,32]{0,1:T(8,128)}, f32[192,32]{0,1:T(8,128)}), (f32[416,32]{0,1:T(8,128)}, f32[192,32]{0,1:T(8,128)})) %all-reduce.17.cloned.1.call-update) | async-done | bytes 77840 | tf_op jit(solution)/shard_map/psum | solution.py:85
  419.2 1.9 fusion.18
  421.1 1.0 fusion.27
  422.2 181.7 %all-reduce.11.cloned.1.call-done = (f32[192,32]{0,1:T(8,128)}, f32[384,32]{0,1:T(8,128)}) async-done(((f32[192,32]{0,1:T(8,128)}, f32[384,32]{0,1:T(8,128)}), (f32[192,32]{0,1:T(8,128)}, f32[384,32]{0,1:T(8,128)})) %all-reduce.11.cloned.1.call-update) | async-done | bytes 73744 | tf_op jit(solution)/shard_map/psum | solution.py:59
  603.9 1.0 fusion.47
  604.9 0.2 fusion.37
  605.1 23.8 %all-reduce.4 = (f32[32,32]{1,0:T(8,128)S(1)}, f32[32,32]{1,0:T(8,128)S(1)}) all-reduce(f32[32,32]{1,0:T(8,128)S(1)} %fusion.47, f32[32,32]{1,0:T(8,128)S(1)} %fusion.37), channel_id=1, replica_groups=mesh['replica'=8,'shard'=8,'tensor'=8] {'shard'}, use_global_device_ids=true, to_apply=%region_5.0 | all-reduce | flops 2048 | bytes 16384 | tf_op jit(solution)/shard_map/psum | solution.py:62
  628.9 0.6 multiply_reduce_fusion.2
  630.7 0.2 fusion.10
  631.0 0.1 fusion.84
  631.1 0.2 fusion.9
  631.4 0.1 fusion.87
  631.6 0.6 multiply_reduce_fusion
  633.4 0.2 fusion.2
  633.7 0.1 fusion.92
  633.8 0.2 fusion.1
  634.1 0.1 fusion.95
  634.3 0.2 fusion.8
  634.6 0.6 copy-done.13
  635.2 0.2 fusion.45
  635.7 0.3 fusion.35
  636.0 1.1 fusion.25
  637.1 1.0 fusion.16
  638.1 185.2 %all-reduce.15.cloned.1.call-done = (f32[416,32]{0,1:T(8,128)}, f32[192,32]{0,1:T(8,128)}) async-done(((f32[416,32]{0,1:T(8,128)}, f32[192,32]{0,1:T(8,128)}), (f32[416,32]{0,1:T(8,128)}, f32[192,32]{0,1:T(8,128)})) %all-reduce.15.cloned.1.call-update) | async-done | bytes 77840 | tf_op jit(solution)/shard_map/psum | solution.py:85
  823.3 0.8 broadcast_multiply_fusion
  824.1 0.8 broadcast_multiply_fusion.1
  824.9 1.4 multiply_subtract_fusion.1
  826.4 1.6 multiply_subtract_fusion
  (67 shorter events, 4.0 us)
Async XLA Ops:
  7.2 0.8 copy-start
  7.2 3.0 copy-start.2
  7.2 2.9 copy-start.4
  7.2 2.9 copy-start.15
  7.2 193.4 %all-reduce.13.cloned.1.call-start = ((), (), s32[]{:S(2)}) async-start(), calls=%async_computation.1 | async-start | bytes 163840 | tf_op jit(solution)/shard_map/psum | solution.py:59
  11.1 408.1 %all-reduce.17.cloned.1.call-start = ((), (), s32[]{:S(2)}) async-start(), calls=%async_computation.3 | async-start | bytes 196608 | tf_op jit(solution)/shard_map/psum | solution.py:85
  200.6 1.0 copy-start.10
  228.1 2.9 copy-start.1
  229.8 0.9 copy-start.14
  229.9 1.2 copy-start.3
  234.0 369.9 %all-reduce.11.cloned.1.call-start = ((), (), s32[]{:S(2)}) async-start(), calls=%async_computation | async-start | bytes 163840 | tf_op jit(solution)/shard_map/psum | solution.py:59
  419.2 1.9 copy-start.16
  422.1 401.1 %all-reduce.15.cloned.1.call-start = ((), (), s32[]{:S(2)}) async-start(), calls=%async_computation.2 | async-start | bytes 196608 | tf_op jit(solution)/shard_map/psum | solution.py:85
  603.9 1.0 copy-start.11
  634.4 0.8 copy-start.13
  637.1 187.8 %copy-start.8 = (f32[384,192]{0,1:T(8,128)S(1)}, f32[384,192]{0,1:T(8,128)}, u32[]{:S(2)}) copy-start(f32[384,192]{0,1:T(8,128)} %param.18) | copy-start | bytes 884740
  638.1 186.8 %copy-start.7 = (f32[384,192]{0,1:T(8,128)S(1)}, f32[384,192]{0,1:T(8,128)}, u32[]{:S(2)}) copy-start(f32[384,192]{0,1:T(8,128)} %param.17) | copy-start | bytes 884740
  824.1 2.2 copy-start.9
  824.9 1.5 copy-start.12
  824.9 1.5 copy-start.5
  824.9 1.5 copy-start.6
Sparse Core Ops, SparseCore 0:
  12.2 188.3 all-reduce.12
  234.2 185.0 all-reduce.16
  423.4 180.4 all-reduce.10
  638.2 185.0 all-reduce.14
where the time goes:
time: 835 us
  waiting for transfers between devices  742 us (89%)
  blocking collectives  47.6 us (6%)
  matrix products  23.3 us (3%)
  between operations  17.1 us (2%)
    psum x2, waiting for transfers between devices, per_device(): lax.psum((partial_in, partial_out), ('replica', 'tensor'))  371 us
    psum x2, waiting for transfers between devices, per_device(): lax.psum((column_in, column_out), ('replica', 'shard'))  370 us
    psum x2, blocking collectives, per_device(): lax.psum((precise_dot(projected_in.T, projected_in), precise_dot(projecte...  47.6 us
    dot_general x58, matrix products, precise_dot(): jnp.dot(left, right, precision=lax.Precision.HIGHEST, preferred_element_t...  19 us
  transfers between devices with their start and end apart: 4, of which 4 were waited for; matrix products, arithmetic and copies ran while one was open for 0% of the time, Pallas kernels for 0%

commit v1 on v0

--- a/solution.py
+++ b/solution.py
@@ -28,6 +28,18 @@
     return inverse / jnp.sqrt(norm_scale)
 
 
+def gather_sum(x, axis):
+    n = lax.axis_size(axis)
+    copies = lax.all_to_all(jnp.broadcast_to(x[None], (n,) + x.shape), axis, 0, 0, tiled=False)
+    return jnp.sum(copies, axis=0)
+
+
+def all_sum(x, axes):
+    for axis in axes:
+        x = gather_sum(x, axis)
+    return x
+
+
 def finish(merged, orthonormal, query, weight, moment):
     approx = precise_dot(orthonormal, query.T)
     residue = (merged - approx)[None]
@@ -49,44 +61,41 @@
     outproj_query,
 ):
     replicas = lax.axis_size("replica")
-    merged_in = inproj_grads[0].astype(jnp.float32) + inproj_error[0]
-    merged_out = outproj_grads[0].astype(jnp.float32) + outproj_error[0]
-    query_in = inproj_query
-    query_out = outproj_query
+    first_replica = (lax.axis_index("replica") == 0).astype(jnp.float32)
+    merged = (
+        inproj_grads[0].astype(jnp.float32) + inproj_error[0],
+        outproj_grads[0].astype(jnp.float32) + outproj_error[0],
+    )
+    rows = [m.shape[0] for m in merged]
+    cols = [m.shape[1] for m in merged]
+    queries = [inproj_query, outproj_query]
     for power_round in range(ROUNDS):
-        partial_in = precise_dot(merged_in, query_in)
-        partial_out = precise_dot(merged_out, query_out)
-        summed_in, summed_out = lax.psum((partial_in, partial_out), ("replica", "tensor"))
-        projected_in = summed_in / replicas
-        projected_out = summed_out / replicas
-        gram_in, gram_out = lax.psum(
-            (
-                precise_dot(projected_in.T, projected_in),
-                precise_dot(projected_out.T, projected_out),
-            ),
-            "shard",
-        )
-        ortho_in = precise_dot(projected_in, inverse_root(gram_in))
-        ortho_out = precise_dot(projected_out, inverse_root(gram_out))
-        column_in = jnp.einsum(
-            "nm,nk->mk",
-            merged_in,
-            ortho_in,
-            precision=lax.Precision.HIGHEST,
-            preferred_element_type=jnp.float32,
-        )
-        column_out = jnp.einsum(
-            "nm,nk->mk",
-            merged_out,
-            ortho_out,
-            precision=lax.Precision.HIGHEST,
-            preferred_element_type=jnp.float32,
-        )
-        summed_cin, summed_cout = lax.psum((column_in, column_out), ("replica", "shard"))
-        query_in = summed_cin / replicas
-        query_out = summed_cout / replicas
-    first = finish(merged_in, ortho_in, query_in, inproj_weight, inproj_moment)
-    second = finish(merged_out, ortho_out, query_out, outproj_weight, outproj_moment)
+        partial = jnp.concatenate([precise_dot(m, q) for m, q in zip(merged, queries)], axis=0)
+        summed = all_sum(partial, ("replica", "tensor")) / replicas
+        projected = [summed[: rows[0]], summed[rows[0] :]]
+        pieces = []
+        for m, p in zip(merged, projected):
+            pieces.append(
+                jnp.einsum(
+                    "nm,nk->mk",
+                    m,
+                    p,
+                    precision=lax.Precision.HIGHEST,
+                    preferred_element_type=jnp.float32,
+                )
+            )
+        for p in projected:
+            pieces.append(precise_dot(p.T, p) * first_replica)
+        column = all_sum(jnp.concatenate(pieces, axis=0), ("replica", "shard"))
+        offsets = [0, cols[0], cols[0] + cols[1]]
+        grams = [column[offsets[2] : offsets[2] + 32], column[offsets[2] + 32 : offsets[2] + 64]]
+        inverses = [inverse_root(g) for g in grams]
+        orthos = [precise_dot(p, z) for p, z in zip(projected, inverses)]
+        queries = [
+            precise_dot(column[offsets[i] : offsets[i + 1]], inverses[i]) / replicas for i in range(2)
+        ]
+    first = finish(merged[0], orthos[0], queries[0], inproj_weight, inproj_moment)
+    second = finish(merged[1], orthos[1], queries[1], outproj_weight, outproj_moment)
     return (first[0], first[1], first[2], first[3], second[0], second[1], second[2], second[3])
 
 

time: 835 us -> 195 us (0.23)
  waiting for transfers between devices: 742 us -> 20.7 us
  blocking collectives: 47.6 us -> 144 us
  between operations: 17.1 us -> 4.21 us
    psum x4 -> x0, waiting for transfers between devices: 741 us -> none  [the longest x2 371 us: per_device(): lax.psum((partial_in, partial_out), ('replica', 'tensor'))]
    all_to_all x0 -> x7, blocking collectives: none -> 144 us  [gather_sum(): lax.all_to_all(jnp.broadcast_to(x[None], (n,) + x.shape), axis, 0, 0, til...]
    psum x2 -> x0, blocking collectives: 47.6 us -> none  [per_device(): lax.psum((precise_dot(projected_in.T, projected_in), precise_dot(projecte...]
    all_to_all x0 -> x1, waiting for transfers between devices: none -> 20.7 us  [gather_sum(): lax.all_to_all(jnp.broadcast_to(x[None], (n,) + x.shape), axis, 0, 0, til...]
    dot_general x58 -> x60, matrix products: 19 us -> 14.9 us  [precise_dot(): jnp.dot(left, right, precision=lax.Precision.HIGHEST, preferred_element_t...]
  transfers between devices with their start and end apart: 4 -> 1, of which waited for: 4 -> 1; matrix products, arithmetic and copies ran while one was open for 0% -> 0% of each run, Pallas kernels for 0% -> 0%
where the time goes in v1:
time: 195 us; the launch traced here: 194 us
  blocking collectives  144 us (74%)
  waiting for transfers between devices  20.7 us (11%)
  matrix products  16.6 us (9%)
  between operations  4.21 us (2%)
  starting transfers between devices  3.54 us (2%)
  local copies, waits for them, and re-layouts  2.91 us (1%)
  other arithmetic  2.03 us (1%)
    all_to_all x7, blocking collectives, gather_sum(): lax.all_to_all(jnp.broadcast_to(x[None], (n,) + x.shape), axis, 0, 0, til...  144 us
    all_to_all x1, waiting for transfers between devices, gather_sum(): lax.all_to_all(jnp.broadcast_to(x[None], (n,) + x.shape), axis, 0, 0, til...  20.7 us
    dot_general x60, matrix products, precise_dot(): jnp.dot(left, right, precision=lax.Precision.HIGHEST, preferred_element_t...  14.9 us
  transfers between devices with their start and end apart: 1, of which 1 were waited for; matrix products, arithmetic and copies ran while one was open for 0% of the time, Pallas kernels for 0%

profile of v1, /device:TPU:1, one launch (start us, length us, event | category | flops | bytes accessed | tf_op | source)
XLA Modules:
  0.0 194.2 jit_solution(15358332669834165419)
XLA Ops:
  0.7 0.8 copy-done
  1.5 1.5 fusion.22
  3.0 0.3 fusion.31
  3.5 20.1 %all_to_all.40 = f32[8,576,32]{1,2,0:T(8,128)S(1)} all-to-all(f32[8,576,32]{1,2,0:T(8,128)S(1)} %broadcast_in_dim.20), channel_id=1, replica_groups=mesh['replica'=8,'shard'=8,'tensor'=8] {'replica'}, dimensions={0} | all-to-all | bytes 1179648 | tf_op jit(solution)/shard_map/all_to_all | solution.py:33
  23.7 0.9 broadcast_in_dim.21
  24.6 3.5 %all-to-all-start.1 = ((f32[8,576,32]{1,2,0:T(8,128)}), f32[8,576,32]{1,2,0:T(8,128)S(1)}, u32[]{:S(2)}, u32[]{:S(2)}) async-start(f32[8,576,32]{1,2,0:T(8,128)} %broadcast_in_dim.21), calls=%async_computation.1 | async-start | bytes 1310720 | tf_op jit(solution)/shard_map/all_to_all | solution.py:33
  28.1 20.7 %all-to-all-done.1 = f32[8,576,32]{1,2,0:T(8,128)S(1)} async-done(((f32[8,576,32]{1,2,0:T(8,128)}), f32[8,576,32]{1,2,0:T(8,128)S(1)}, u32[]{:S(2)}, u32[]{:S(2)}) %all-to-all-start.1) | async-done | bytes 589856 | tf_op jit(solution)/shard_map/all_to_all | solution.py:33
  48.9 0.2 convolution_multiply_fusion.7
  49.0 0.3 convolution_multiply_fusion.6
  49.3 0.5 fusion.29
  49.8 0.4 copy-done.3
  50.3 0.4 fusion.20
  50.8 15.0 %all_to_all.41 = f32[8,672,32]{1,2,0:T(8,128)S(1)} all-to-all(f32[8,672,32]{1,2,0:T(8,128)S(1)} %broadcast_in_dim.22), channel_id=1, replica_groups=mesh['replica'=8,'shard'=8,'tensor'=8] {'replica'}, dimensions={0} | all-to-all | bytes 1376256 | tf_op jit(solution)/shard_map/all_to_all | solution.py:33
  65.9 30.9 %all_to_all.42 = f32[8,672,32]{1,2,0:T(8,128)S(1)} all-to-all(f32[8,672,32]{1,2,0:T(8,128)S(1)} %broadcast_in_dim.23), channel_id=1, replica_groups=mesh['replica'=8,'shard'=8,'tensor'=8] {'shard'}, dimensions={0} | all-to-all | bytes 1376256 | tf_op jit(solution)/shard_map/all_to_all | solution.py:33
  96.9 0.7 multiply_reduce_fusion.3
  98.3 0.2 fusion.15
  98.5 0.3 fusion.54
  99.4 0.2 fusion.13
  100.8 0.2 fusion.55
  101.6 0.2 fusion.9
  102.0 0.2 fusion.8
  102.3 0.3 convolution_multiply_fusion.3
  102.9 0.3 convolution_multiply_fusion.1
  103.2 0.5 fusion.18
  103.6 0.3 fusion.27
  104.1 16.0 %all_to_all.43 = f32[8,576,32]{1,2,0:T(8,128)S(1)} all-to-all(f32[8,576,32]{1,2,0:T(8,128)S(1)} %broadcast_in_dim.24), channel_id=1, replica_groups=mesh['replica'=8,'shard'=8,'tensor'=8] {'replica'}, dimensions={0} | all-to-all | bytes 1179648 | tf_op jit(solution)/shard_map/all_to_all | solution.py:33
  120.2 21.5 %all_to_all.44 = f32[8,576,32]{1,2,0:T(8,128)S(1)} all-to-all(f32[8,576,32]{1,2,0:T(8,128)S(1)} %broadcast_in_dim.25), channel_id=1, replica_groups=mesh['replica'=8,'shard'=8,'tensor'=8] {'tensor'}, dimensions={0} | all-to-all | bytes 1179648 | tf_op jit(solution)/shard_map/all_to_all | solution.py:33
  141.8 0.2 convolution_multiply_fusion.5
  141.9 0.3 convolution_multiply_fusion.4
  142.2 0.5 fusion.25
  142.7 0.4 fusion.16
  143.2 16.7 %all_to_all.45 = f32[8,672,32]{1,2,0:T(8,128)S(1)} all-to-all(f32[8,672,32]{1,2,0:T(8,128)S(1)} %broadcast_in_dim.26), channel_id=1, replica_groups=mesh['replica'=8,'shard'=8,'tensor'=8] {'replica'}, dimensions={0} | all-to-all | bytes 1376256 | tf_op jit(solution)/shard_map/all_to_all | solution.py:33
  160.0 24.0 %all_to_all.46 = f32[8,672,32]{1,2,0:T(8,128)S(1)} all-to-all(f32[8,672,32]{1,2,0:T(8,128)S(1)} %broadcast_in_dim.27), channel_id=1, replica_groups=mesh['replica'=8,'shard'=8,'tensor'=8] {'shard'}, dimensions={0} | all-to-all | bytes 1376256 | tf_op jit(solution)/shard_map/all_to_all | solution.py:33
  184.1 0.7 multiply_reduce_fusion
  185.6 0.2 fusion.57
  186.0 0.2 fusion.2
  186.4 0.2 fusion.1
  187.6 0.2 fusion.7
  187.8 0.3 fusion.56
  188.3 0.2 fusion.6
  188.7 0.2 fusion.5
  189.5 0.3 convolution_multiply_fusion
  189.8 0.2 fusion.46
  190.3 0.3 convolution_multiply_fusion.2
  190.6 0.3 fusion.38
  190.8 0.3 copy-done.10
  191.2 1.4 multiply_subtract_fusion.1
  192.6 1.6 multiply_subtract_fusion
  (73 shorter events, 5.5 us)
Async XLA Ops:
  0.6 0.8 copy-start
  0.6 2.3 %copy-start.2 = (f32[1,384,192]{1,2,0:T(8,128)S(1)}, f32[1,384,192]{1,2,0:T(8,128)}, u32[]{:S(2)}) copy-start(f32[1,384,192]{1,2,0:T(8,128)} %param.16) | copy-start | bytes 884740
  0.7 2.3 %copy-start.4 = (bf16[1,384,192]{1,2,0:T(8,128)(2,1)S(1)}, bf16[1,384,192]{1,2,0:T(8,128)(2,1)}, u32[]{:S(2)}) copy-start(bf16[1,384,192]{1,2,0:T(8,128)(2,1)} %param.15) | copy-start | bytes 442372
  0.7 2.3 %copy-start.11 = (f32[192,32]{0,1:T(8,128)S(1)}, f32[192,32]{0,1:T(8,128)}, u32[]{:S(2)}) copy-start(f32[192,32]{0,1:T(8,128)} %param.19) | copy-start | bytes 73732
  24.6 24.2 %all-to-all-start.1 = ((f32[8,576,32]{1,2,0:T(8,128)}), f32[8,576,32]{1,2,0:T(8,128)S(1)}, u32[]{:S(2)}, u32[]{:S(2)}) async-start(f32[8,576,32]{1,2,0:T(8,128)} %broadcast_in_dim.21), calls=%async_computation.1 | async-start | bytes 1310720 | tf_op jit(solution)/shard_map/all_to_all | solution.py:33
  48.8 1.0 copy-start.1
  49.3 1.0 copy-start.3
  189.2 2.0 %copy-start.8 = (f32[384,192]{0,1:T(8,128)S(1)}, f32[384,192]{0,1:T(8,128)}, u32[]{:S(2)}) copy-start(f32[384,192]{0,1:T(8,128)} %param.18) | copy-start | bytes 884740
  189.3 1.8 copy-start.7
  189.8 2.8 %copy-start.9 = (f32[416,32]{0,1:T(8,128)}, f32[416,32]{0,1:T(8,128)S(1)}, u32[]{:S(2)}) copy-start(f32[416,32]{0,1:T(8,128)S(1)} %convolution_multiply_fusion) | copy-start | bytes 159748
  190.6 0.6 copy-start.10
  191.2 1.4 copy-start.5
  191.2 1.4 copy-start.6

commit v2 on v1

--- a/solution.py
+++ b/solution.py
@@ -48,6 +48,27 @@
     return (master, velocity, residue, query)
 
 
+def replica_total(blocks):
+    n = lax.axis_size("replica")
+    d = 1
+    while d < n:
+        pairs = [(i, i ^ d) for i in range(n)]
+        moved = lax.ppermute(blocks, "replica", pairs)
+        blocks = tuple(b + m for b, m in zip(blocks, moved))
+        d *= 2
+    return blocks
+
+
+def contract_rows(m, p):
+    return jnp.einsum(
+        "nm,nk->mk",
+        m,
+        p,
+        precision=lax.Precision.HIGHEST,
+        preferred_element_type=jnp.float32,
+    )
+
+
 def per_device(
     inproj_grads,
     inproj_error,
@@ -66,29 +87,24 @@
         inproj_grads[0].astype(jnp.float32) + inproj_error[0],
         outproj_grads[0].astype(jnp.float32) + outproj_error[0],
     )
+    total = replica_total(merged)
     rows = [m.shape[0] for m in merged]
     cols = [m.shape[1] for m in merged]
+    rank = inproj_query.shape[1]
     queries = [inproj_query, outproj_query]
     for power_round in range(ROUNDS):
-        partial = jnp.concatenate([precise_dot(m, q) for m, q in zip(merged, queries)], axis=0)
-        summed = all_sum(partial, ("replica", "tensor")) / replicas
+        if power_round == 0:
+            source, row_axes, col_axes, gram_weight = merged, ("replica", "tensor"), ("replica", "shard"), first_replica
+        else:
+            source, row_axes, col_axes, gram_weight = total, ("tensor",), ("shard",), 1.0
+        partial = jnp.concatenate([precise_dot(m, q) for m, q in zip(source, queries)], axis=0)
+        summed = all_sum(partial, row_axes) / replicas
         projected = [summed[: rows[0]], summed[rows[0] :]]
-        pieces = []
-        for m, p in zip(merged, projected):
-            pieces.append(
-                jnp.einsum(
-                    "nm,nk->mk",
-                    m,
-                    p,
-                    precision=lax.Precision.HIGHEST,
-                    preferred_element_type=jnp.float32,
-                )
-            )
-        for p in projected:
-            pieces.append(precise_dot(p.T, p) * first_replica)
-        column = all_sum(jnp.concatenate(pieces, axis=0), ("replica", "shard"))
+        pieces = [contract_rows(m, p) for m, p in zip(source, projected)]
+        pieces += [precise_dot(p.T, p) * gram_weight for p in projected]
+        column = all_sum(jnp.concatenate(pieces, axis=0), col_axes)
         offsets = [0, cols[0], cols[0] + cols[1]]
-        grams = [column[offsets[2] : offsets[2] + 32], column[offsets[2] + 32 : offsets[2] + 64]]
+        grams = [column[offsets[2] : offsets[2] + rank], column[offsets[2] + rank : offsets[2] + 2 * rank]]
         inverses = [inverse_root(g) for g in grams]
         orthos = [precise_dot(p, z) for p, z in zip(projected, inverses)]
         queries = [

time: 195 us -> 185 us (0.949)
  blocking collectives: 144 us -> 83.4 us
  starting transfers between devices: 3.54 us -> 29.3 us
  waiting for transfers between devices: 20.7 us -> 43.2 us
    all_to_all x7 -> x4, blocking collectives: 144 us -> 83.4 us  [gather_sum(): lax.all_to_all(jnp.broadcast_to(x[None], (n,) + x.shape), axis, 0, 0, til...]
    ppermute x0 -> x6, waiting for transfers between devices: none -> 22.6 us  [replica_total(): moved = lax.ppermute(blocks, 'replica', pairs)]
    ppermute x0 -> x6, starting transfers between devices: none -> 16 us  [replica_total(): moved = lax.ppermute(blocks, 'replica', pairs)]
    all_to_all x1 -> x2, starting transfers between devices: 3.54 us -> 13.3 us  [gather_sum(): lax.all_to_all(jnp.broadcast_to(x[None], (n,) + x.shape), axis, 0, 0, til...]
    all_to_all x1 -> x2, waiting for transfers between devices: 20.7 us -> 20.7 us  [gather_sum(): lax.all_to_all(jnp.broadcast_to(x[None], (n,) + x.shape), axis, 0, 0, til...]
  transfers between devices with their start and end apart: 1 -> 8, of which waited for: 1 -> 4; matrix products, arithmetic and copies ran while one was open for 0% -> 0% of each run, Pallas kernels for 0% -> 0%
where the time goes in v2:
time: 185 us; the launch traced here: 182 us
  blocking collectives  83.4 us (45%)
  waiting for transfers between devices  43.2 us (23%)
  starting transfers between devices  29.3 us (16%)
  matrix products  15.4 us (8%)
  between operations  4.37 us (2%)
  other arithmetic  3.37 us (2%)
  local copies, waits for them, and re-layouts  3.33 us (2%)
    all_to_all x4, blocking collectives, gather_sum(): lax.all_to_all(jnp.broadcast_to(x[None], (n,) + x.shape), axis, 0, 0, til...  83.4 us
    ppermute x6, waiting for transfers between devices, replica_total(): moved = lax.ppermute(blocks, 'replica', pairs)  22.6 us
    all_to_all x2, waiting for transfers between devices, gather_sum(): lax.all_to_all(jnp.broadcast_to(x[None], (n,) + x.shape), axis, 0, 0, til...  20.7 us
    ppermute x6, starting transfers between devices, replica_total(): moved = lax.ppermute(blocks, 'replica', pairs)  16 us
    dot_general x60, matrix products, precise_dot(): jnp.dot(left, right, precision=lax.Precision.HIGHEST, preferred_element_t...  13.8 us
    all_to_all x2, starting transfers between devices, gather_sum(): lax.all_to_all(jnp.broadcast_to(x[None], (n,) + x.shape), axis, 0, 0, til...  13.3 us
  transfers between devices with their start and end apart: 8, of which 4 were waited for; matrix products, arithmetic and copies ran while one was open for 0% of the time, Pallas kernels for 0%

profile of v2, /device:TPU:1, one launch (start us, length us, event | category | flops | bytes accessed | tf_op | source)
XLA Modules:
  0.0 182.5 jit_solution(10206067849380434381)
XLA Ops:
  0.6 1.1 add_bitcast_fusion
  1.8 0.5 fusion.46
  2.3 0.5 copy-done.5
  2.8 0.7 copy-done.9
  3.5 0.3 fusion.47
  4.0 20.1 %all_to_all.30 = f32[8,576,32]{1,2,0:T(8,128)S(1)} all-to-all(f32[8,576,32]{1,2,0:T(8,128)S(1)} %broadcast_in_dim.16), channel_id=1, replica_groups=mesh['replica'=8,'shard'=8,'tensor'=8] {'replica'}, dimensions={0} | all-to-all | bytes 1179648 | tf_op jit(solution)/shard_map/all_to_all | solution.py:33
  24.2 0.9 broadcast_in_dim.17
  25.1 3.5 %all-to-all-start.1 = ((f32[8,576,32]{1,2,0:T(8,128)}), f32[8,576,32]{1,2,0:T(8,128)S(1)}, u32[]{:S(2)}, u32[]{:S(2)}) async-start(f32[8,576,32]{1,2,0:T(8,128)} %broadcast_in_dim.17), calls=%async_computation.1 | async-start | bytes 1310720 | tf_op jit(solution)/shard_map/all_to_all | solution.py:33
  28.6 20.7 %all-to-all-done.1 = f32[8,576,32]{1,2,0:T(8,128)S(1)} async-done(((f32[8,576,32]{1,2,0:T(8,128)}), f32[8,576,32]{1,2,0:T(8,128)S(1)}, u32[]{:S(2)}, u32[]{:S(2)}) %all-to-all-start.1) | async-done | bytes 589856 | tf_op jit(solution)/shard_map/all_to_all | solution.py:33
  49.4 0.3 fusion.30
  49.7 0.5 fusion.19
  50.2 0.3 convolution_multiply_fusion.4
  50.5 0.2 convolution_multiply_fusion.5
  50.8 15.0 %all_to_all.31 = f32[8,672,32]{1,2,0:T(8,128)S(1)} all-to-all(f32[8,672,32]{1,2,0:T(8,128)S(1)} %broadcast_in_dim.18), channel_id=1, replica_groups=mesh['replica'=8,'shard'=8,'tensor'=8] {'replica'}, dimensions={0} | all-to-all | bytes 1376256 | tf_op jit(solution)/shard_map/all_to_all | solution.py:33
  65.9 0.9 broadcast_in_dim.19
  66.8 9.8 %all-to-all-start.3 = ((f32[8,672,32]{1,2,0:T(8,128)}), f32[8,672,32]{1,2,0:T(8,128)S(1)}, u32[]{:S(2)}, u32[]{:S(2)}) async-start(f32[8,672,32]{1,2,0:T(8,128)} %broadcast_in_dim.19), calls=%async_computation.3 | async-start | bytes 1572864 | tf_op jit(solution)/shard_map/all_to_all | solution.py:33
  76.6 3.2 %collective-permute-start = (f32[192,416]{1,0:T(8,128)S(1)}, f32[192,416]{1,0:T(8,128)S(1)}, u32[]{:S(2)}, u32[]{:S(2)}) collective-permute-start(f32[192,416]{1,0:T(8,128)S(1)} %add_bitcast_fusion), channel_id=1, source_target_pairs={{0,64},{64,0},{128,192},{192,128},{256,320},{320,256},{384,448},{4... | collective-permute-start | bytes 958472 | tf_op jit(solution)/shard_map/ppermute | solution.py:56
  79.8 1.9 %collective-permute-start.3 = (f32[384,192]{0,1:T(8,128)S(1)}, f32[384,192]{0,1:T(8,128)S(1)}, u32[]{:S(2)}, u32[]{:S(2)}) collective-permute-start(f32[384,192]{0,1:T(8,128)S(1)} %add_bitcast_fusion.1), channel_id=1, source_target_pairs={{0,64},{64,0},{128,192},{192,128},{256,320},{320,256},{384,448},{4... | collective-permute-start | bytes 884744 | tf_op jit(solution)/shard_map/ppermute | solution.py:56
  81.8 2.2 %collective-permute-start.1 = (f32[192,416]{1,0:T(8,128)S(1)}, f32[192,416]{1,0:T(8,128)S(1)}, u32[]{:S(2)}, u32[]{:S(2)}) collective-permute-start(f32[192,416]{1,0:T(8,128)S(1)} %add.50), channel_id=1, source_target_pairs={{0,128},{64,192},{128,0},{192,64},{256,384},{320,448},{384,256},{4... | collective-permute-start | bytes 958472 | tf_op jit(solution)/shard_map/ppermute | solution.py:56
  84.1 3.0 %collective-permute-start.4 = (f32[384,192]{0,1:T(8,128)S(1)}, f32[384,192]{0,1:T(8,128)S(1)}, u32[]{:S(2)}, u32[]{:S(2)}) collective-permute-start(f32[384,192]{0,1:T(8,128)S(1)} %add.56), channel_id=1, source_target_pairs={{0,128},{64,192},{128,0},{192,64},{256,384},{320,448},{384,256},{4... | collective-permute-start | bytes 884744 | tf_op jit(solution)/shard_map/ppermute | solution.py:56
  87.2 6.7 %collective-permute-done.1 = f32[192,416]{1,0:T(8,128)S(1)} collective-permute-done((f32[192,416]{1,0:T(8,128)S(1)}, f32[192,416]{1,0:T(8,128)S(1)}, u32[]{:S(2)}, u32[]{:S(2)}) %collective-permute-start.1) | collective-permute-done | bytes 319520 | tf_op jit(solution)/shard_map/ppermute | solution.py:56
  94.0 2.8 %collective-permute-start.2 = (f32[192,416]{1,0:T(8,128)S(1)}, f32[192,416]{1,0:T(8,128)S(1)}, u32[]{:S(2)}, u32[]{:S(2)}) collective-permute-start(f32[192,416]{1,0:T(8,128)S(1)} %add.51), channel_id=1, source_target_pairs={{0,256},{64,320},{128,384},{192,448},{256,0},{320,64},{384,128},{4... | collective-permute-start | bytes 958472 | tf_op jit(solution)/shard_map/ppermute | solution.py:56
  96.8 3.5 %collective-permute-done.4 = f32[384,192]{0,1:T(8,128)S(1)} collective-permute-done((f32[384,192]{0,1:T(8,128)S(1)}, f32[384,192]{0,1:T(8,128)S(1)}, u32[]{:S(2)}, u32[]{:S(2)}) %collective-permute-start.4) | collective-permute-done | bytes 294944 | tf_op jit(solution)/shard_map/ppermute | solution.py:56
  100.2 2.8 %collective-permute-start.5 = (f32[384,192]{0,1:T(8,128)S(1)}, f32[384,192]{0,1:T(8,128)S(1)}, u32[]{:S(2)}, u32[]{:S(2)}) collective-permute-start(f32[384,192]{0,1:T(8,128)S(1)} %add.57), channel_id=1, source_target_pairs={{0,256},{64,320},{128,384},{192,448},{256,0},{320,64},{384,128},{4... | collective-permute-start | bytes 884744 | tf_op jit(solution)/shard_map/ppermute | solution.py:56
  103.0 12.4 %collective-permute-done.5 = f32[384,192]{0,1:T(8,128)S(1)} collective-permute-done((f32[384,192]{0,1:T(8,128)S(1)}, f32[384,192]{0,1:T(8,128)S(1)}, u32[]{:S(2)}, u32[]{:S(2)}) %collective-permute-start.5) | collective-permute-done | bytes 294944 | tf_op jit(solution)/shard_map/ppermute | solution.py:56
  115.6 0.7 multiply_reduce_fusion.3
  117.0 0.2 fusion.15
  117.2 0.3 fusion.42
  119.4 0.2 fusion.43
  121.1 0.3 convolution_multiply_fusion.1
  121.6 0.3 convolution_multiply_fusion.3
  121.9 0.5 fusion.52
  122.4 0.3 fusion.57
  122.8 21.4 %all_to_all.32 = f32[8,576,32]{1,2,0:T(8,128)S(1)} all-to-all(f32[8,576,32]{1,2,0:T(8,128)S(1)} %broadcast_in_dim.20), channel_id=1, replica_groups=mesh['replica'=8,'shard'=8,'tensor'=8] {'tensor'}, dimensions={0} | all-to-all | bytes 1179648 | tf_op jit(solution)/shard_map/all_to_all | solution.py:33
  144.3 0.3 fusion.36
  144.6 0.5 fusion.25
  145.1 0.3 fusion.23
  145.7 26.9 %all_to_all.33 = f32[8,672,32]{1,2,0:T(8,128)S(1)} all-to-all(f32[8,672,32]{1,2,0:T(8,128)S(1)} %broadcast_in_dim.21), channel_id=1, replica_groups=mesh['replica'=8,'shard'=8,'tensor'=8] {'shard'}, dimensions={0} | all-to-all | bytes 1376256 | tf_op jit(solution)/shard_map/all_to_all | solution.py:33
  172.6 0.7 multiply_reduce_fusion
  174.1 0.2 fusion.45
  175.7 0.3 convolution_multiply_fusion.2
  176.0 0.3 fusion.21
  177.0 0.2 fusion.7
  177.2 0.3 fusion.44
  178.9 0.3 convolution_multiply_fusion
  179.2 0.2 fusion.32
  179.5 1.4 multiply_subtract_fusion.1
  180.8 1.6 multiply_subtract_fusion
  (84 shorter events, 6.8 us)
Async XLA Ops:
  0.6 1.1 copy-start
  1.8 1.0 copy-start.5
  1.8 1.0 copy-start.7
  2.8 0.8 copy-start.9
  25.1 24.2 %all-to-all-start.1 = ((f32[8,576,32]{1,2,0:T(8,128)}), f32[8,576,32]{1,2,0:T(8,128)S(1)}, u32[]{:S(2)}, u32[]{:S(2)}) async-start(f32[8,576,32]{1,2,0:T(8,128)} %broadcast_in_dim.17), calls=%async_computation.1 | async-start | bytes 1310720 | tf_op jit(solution)/shard_map/all_to_all | solution.py:33
  66.8 48.7 %all-to-all-start.3 = ((f32[8,672,32]{1,2,0:T(8,128)}), f32[8,672,32]{1,2,0:T(8,128)S(1)}, u32[]{:S(2)}, u32[]{:S(2)}) async-start(f32[8,672,32]{1,2,0:T(8,128)} %broadcast_in_dim.19), calls=%async_computation.3 | async-start | bytes 1572864 | tf_op jit(solution)/shard_map/all_to_all | solution.py:33
  76.6 5.2 %collective-permute-start = (f32[192,416]{1,0:T(8,128)S(1)}, f32[192,416]{1,0:T(8,128)S(1)}, u32[]{:S(2)}, u32[]{:S(2)}) collective-permute-start(f32[192,416]{1,0:T(8,128)S(1)} %add_bitcast_fusion), channel_id=1, source_target_pairs={{0,64},{64,0},{128,192},{192,128},{256,320},{320,256},{384,448},{4... | collective-permute-start | bytes 958472 | tf_op jit(solution)/shard_map/ppermute | solution.py:56
  79.8 4.2 %collective-permute-start.3 = (f32[384,192]{0,1:T(8,128)S(1)}, f32[384,192]{0,1:T(8,128)S(1)}, u32[]{:S(2)}, u32[]{:S(2)}) collective-permute-start(f32[384,192]{0,1:T(8,128)S(1)} %add_bitcast_fusion.1), channel_id=1, source_target_pairs={{0,64},{64,0},{128,192},{192,128},{256,320},{320,256},{384,448},{4... | collective-permute-start | bytes 884744 | tf_op jit(solution)/shard_map/ppermute | solution.py:56
  81.8 12.1 %collective-permute-start.1 = (f32[192,416]{1,0:T(8,128)S(1)}, f32[192,416]{1,0:T(8,128)S(1)}, u32[]{:S(2)}, u32[]{:S(2)}) collective-permute-start(f32[192,416]{1,0:T(8,128)S(1)} %add.50), channel_id=1, source_target_pairs={{0,128},{64,192},{128,0},{192,64},{256,384},{320,448},{384,256},{4... | collective-permute-start | bytes 958472 | tf_op jit(solution)/shard_map/ppermute | solution.py:56
  84.1 16.1 %collective-permute-start.4 = (f32[384,192]{0,1:T(8,128)S(1)}, f32[384,192]{0,1:T(8,128)S(1)}, u32[]{:S(2)}, u32[]{:S(2)}) collective-permute-start(f32[384,192]{0,1:T(8,128)S(1)} %add.56), channel_id=1, source_target_pairs={{0,128},{64,192},{128,0},{192,64},{256,384},{320,448},{384,256},{4... | collective-permute-start | bytes 884744 | tf_op jit(solution)/shard_map/ppermute | solution.py:56
  94.0 21.5 %collective-permute-start.2 = (f32[192,416]{1,0:T(8,128)S(1)}, f32[192,416]{1,0:T(8,128)S(1)}, u32[]{:S(2)}, u32[]{:S(2)}) collective-permute-start(f32[192,416]{1,0:T(8,128)S(1)} %add.51), channel_id=1, source_target_pairs={{0,256},{64,320},{128,384},{192,448},{256,0},{320,64},{384,128},{4... | collective-permute-start | bytes 958472 | tf_op jit(solution)/shard_map/ppermute | solution.py:56
  100.2 15.2 %collective-permute-start.5 = (f32[384,192]{0,1:T(8,128)S(1)}, f32[384,192]{0,1:T(8,128)S(1)}, u32[]{:S(2)}, u32[]{:S(2)}) collective-permute-start(f32[384,192]{0,1:T(8,128)S(1)} %add.57), channel_id=1, source_target_pairs={{0,256},{64,320},{128,384},{192,448},{256,0},{320,64},{384,128},{4... | collective-permute-start | bytes 884744 | tf_op jit(solution)/shard_map/ppermute | solution.py:56
  176.0 3.4 %copy-start.8 = (f32[192,32]{0,1:T(8,128)}, f32[192,32]{0,1:T(8,128)S(1)}, u32[]{:S(2)}) copy-start(f32[192,32]{0,1:T(8,128)S(1)} %convolution_multiply_fusion.2) | copy-start | bytes 73732
  177.6 1.8 copy-start.4
  177.8 1.6 copy-start.3
  179.2 1.7 copy-start.6
  179.4 1.4 copy-start.1
  179.4 1.4 copy-start.2

commit v3 on v2

--- a/solution.py
+++ b/solution.py
@@ -2,6 +2,7 @@
 import jax.numpy as jnp
 from jax import lax
 from jax.sharding import PartitionSpec as P
+
 
 ROUNDS = 2
 NS_STEPS = 4
@@ -16,15 +17,25 @@
     return jnp.dot(left, right, precision=lax.Precision.HIGHEST, preferred_element_type=jnp.float32)
 
 
+def batched_dot(left, right):
+    return jnp.einsum(
+        "bij,bjk->bik",
+        left,
+        right,
+        precision=lax.Precision.HIGHEST,
+        preferred_element_type=jnp.float32,
+    )
+
+
 def inverse_root(gram_sum):
-    identity = jnp.eye(gram_sum.shape[0], dtype=jnp.float32)
-    norm_scale = jnp.sqrt(jnp.sum(gram_sum * gram_sum) + EPSILON)
+    identity = jnp.eye(gram_sum.shape[-1], dtype=jnp.float32)[None]
+    norm_scale = jnp.sqrt(jnp.sum(gram_sum * gram_sum, axis=(1, 2), keepdims=True) + EPSILON)
     current = gram_sum / norm_scale
-    inverse = identity
-    for sweep in range(NS_STEPS):
-        middle = 0.5 * (3.0 * identity - precise_dot(inverse, current))
-        current = precise_dot(current, middle)
-        inverse = precise_dot(middle, inverse)
+    inverse = jnp.broadcast_to(identity, gram_sum.shape)
+    for _ in range(NS_STEPS):
+        middle = 0.5 * (3.0 * identity - batched_dot(inverse, current))
+        current = batched_dot(current, middle)
+        inverse = batched_dot(middle, inverse)
     return inverse / jnp.sqrt(norm_scale)
 
 
@@ -48,15 +59,18 @@
     return (master, velocity, residue, query)
 
 
-def replica_total(blocks):
+def replica_total(blocks, order):
     n = lax.axis_size("replica")
-    d = 1
-    while d < n:
+    height = blocks[0].shape[0]
+    flat = jnp.concatenate([b.reshape(height, -1) for b in blocks], axis=1)
+    for d in order:
         pairs = [(i, i ^ d) for i in range(n)]
-        moved = lax.ppermute(blocks, "replica", pairs)
-        blocks = tuple(b + m for b, m in zip(blocks, moved))
-        d *= 2
-    return blocks
+        moved = lax.ppermute(flat, "replica", pairs)
+        flat = flat + moved
+    widths = [b.size // height for b in blocks]
+    first = flat[:, : widths[0]].reshape(blocks[0].shape)
+    second = flat[:, widths[0] :].reshape(blocks[1].shape)
+    return (first, second)
 
 
 def contract_rows(m, p):
@@ -82,31 +96,30 @@
     outproj_query,
 ):
     replicas = lax.axis_size("replica")
-    first_replica = (lax.axis_index("replica") == 0).astype(jnp.float32)
     merged = (
         inproj_grads[0].astype(jnp.float32) + inproj_error[0],
         outproj_grads[0].astype(jnp.float32) + outproj_error[0],
     )
-    total = replica_total(merged)
+    total = replica_total(merged, (2, 4, 1))
     rows = [m.shape[0] for m in merged]
     cols = [m.shape[1] for m in merged]
     rank = inproj_query.shape[1]
     queries = [inproj_query, outproj_query]
     for power_round in range(ROUNDS):
         if power_round == 0:
-            source, row_axes, col_axes, gram_weight = merged, ("replica", "tensor"), ("replica", "shard"), first_replica
+            rows_source, row_axes = merged, ("replica", "tensor")
         else:
-            source, row_axes, col_axes, gram_weight = total, ("tensor",), ("shard",), 1.0
-        partial = jnp.concatenate([precise_dot(m, q) for m, q in zip(source, queries)], axis=0)
+            rows_source, row_axes = total, ("tensor",)
+        partial = jnp.concatenate([precise_dot(m, q) for m, q in zip(rows_source, queries)], axis=0)
         summed = all_sum(partial, row_axes) / replicas
         projected = [summed[: rows[0]], summed[rows[0] :]]
-        pieces = [contract_rows(m, p) for m, p in zip(source, projected)]
-        pieces += [precise_dot(p.T, p) * gram_weight for p in projected]
-        column = all_sum(jnp.concatenate(pieces, axis=0), col_axes)
+        pieces = [contract_rows(m, p) for m, p in zip(total, projected)]
+        pieces += [precise_dot(p.T, p) for p in projected]
+        column = all_sum(jnp.concatenate(pieces, axis=0), ("shard",))
         offsets = [0, cols[0], cols[0] + cols[1]]
-        grams = [column[offsets[2] : offsets[2] + rank], column[offsets[2] + rank : offsets[2] + 2 * rank]]
-        inverses = [inverse_root(g) for g in grams]
-        orthos = [precise_dot(p, z) for p, z in zip(projected, inverses)]
+        grams = column[offsets[2] :].reshape(2, rank, rank)
+        inverses = inverse_root(grams)
+        orthos = [precise_dot(p, inverses[i]) for i, p in enumerate(projected)]
         queries = [
             precise_dot(column[offsets[i] : offsets[i + 1]], inverses[i]) / replicas for i in range(2)
         ]

time: 185 us -> 159 us (0.86)
  blocking collectives: 83.4 us -> 48.5 us
  waiting for transfers between devices: 43.2 us -> 55 us
  between operations: 4.37 us -> 1.23 us
  matrix products: 15.4 us -> 12.3 us
    all_to_all x4 -> x2, blocking collectives: 83.4 us -> 48.5 us  [gather_sum(): lax.all_to_all(jnp.broadcast_to(x[None], (n,) + x.shape), axis, 0, 0, til...]
    all_to_all x2 -> x3, waiting for transfers between devices: 20.7 us -> 29.8 us  [gather_sum(): lax.all_to_all(jnp.broadcast_to(x[None], (n,) + x.shape), axis, 0, 0, til...]
    dot_general x60 -> x16, matrix products: 13.8 us -> 7.05 us  [precise_dot(): jnp.dot(left, right, precision=lax.Precision.HIGHEST, preferred_element_t...]
    all_to_all x2 -> x3, starting transfers between devices: 13.3 us -> 19.3 us  [gather_sum(): lax.all_to_all(jnp.broadcast_to(x[None], (n,) + x.shape), axis, 0, 0, til...]
    ppermute x6 -> x3, starting transfers between devices: 16 us -> 11.3 us  [replica_total(): moved = lax.ppermute(flat, 'replica', pairs)]
    dot_general x0 -> x22, matrix products: none -> 3.88 us  [batched_dot(): jnp.einsum('bij,bjk->bik', left, right, precision=lax.Precision.HIGHEST,...]
    ppermute x6 -> x3, waiting for transfers between devices: 22.6 us -> 25.2 us  [replica_total(): moved = lax.ppermute(flat, 'replica', pairs)]
  transfers between devices with their start and end apart: 8 -> 6, of which waited for: 4 -> 5; matrix products, arithmetic and copies ran while one was open for 0% -> 2% of each run, Pallas kernels for 0% -> 0%
where the time goes in v3:
time: 159 us; the launch traced here: 156 us
  waiting for transfers between devices  55 us (35%)
  blocking collectives  48.5 us (31%)
  starting transfers between devices  30.7 us (19%)
  matrix products  12.3 us (8%)
  other arithmetic  4.58 us (3%)
  local copies, waits for them, and re-layouts  4.22 us (3%)
    all_to_all x2, blocking collectives, gather_sum(): lax.all_to_all(jnp.broadcast_to(x[None], (n,) + x.shape), axis, 0, 0, til...  48.5 us
    all_to_all x3, waiting for transfers between devices, gather_sum(): lax.all_to_all(jnp.broadcast_to(x[None], (n,) + x.shape), axis, 0, 0, til...  29.8 us
    ppermute x3, waiting for transfers between devices, replica_total(): moved = lax.ppermute(flat, 'replica', pairs)  25.2 us
    all_to_all x3, starting transfers between devices, gather_sum(): lax.all_to_all(jnp.broadcast_to(x[None], (n,) + x.shape), axis, 0, 0, til...  19.3 us
    ppermute x3, starting transfers between devices, replica_total(): moved = lax.ppermute(flat, 'replica', pairs)  11.3 us
    dot_general x16, matrix products, precise_dot(): jnp.dot(left, right, precision=lax.Precision.HIGHEST, preferred_element_t...  7.05 us
    dot_general x22, matrix products, batched_dot(): jnp.einsum('bij,bjk->bik', left, right, precision=lax.Precision.HIGHEST,...  3.88 us
  transfers between devices with their start and end apart: 6, of which 5 were waited for; matrix products, arithmetic and copies ran while one was open for 2% of the time, Pallas kernels for 0%

profile of v3, /device:TPU:1, one launch (start us, length us, event | category | flops | bytes accessed | tf_op | source)
XLA Modules:
  0.0 156.4 jit_solution(14173359959475906254)
XLA Ops:
  0.7 1.1 convert_add_fusion
  1.8 0.2 copy-done.3
  2.0 0.5 fusion.52
  2.5 0.3 copy-done.9
  2.8 0.3 fusion.14
  3.2 0.9 broadcast_in_dim.22
  4.1 10.3 %all-to-all-start = ((f32[8,576,32]{1,2,0:T(8,128)}), f32[8,576,32]{1,2,0:T(8,128)S(1)}, u32[]{:S(2)}, u32[]{:S(2)}) async-start(f32[8,576,32]{1,2,0:T(8,128)} %broadcast_in_dim.22), calls=%async_computation | async-start | bytes 1310720 | tf_op jit(solution)/shard_map/all_to_all | solution.py:44
  14.7 1.0 pad_maximum_fusion
  15.7 3.3 %collective-permute-start = (f32[192,800]{1,0:T(8,128)}, f32[192,800]{1,0:T(8,128)S(1)}, u32[]{:S(2)}, u32[]{:S(2)}) collective-permute-start(f32[192,800]{1,0:T(8,128)} %pad_maximum_fusion), channel_id=1, source_target_pairs={{0,128},{64,192},{128,0},{192,64},{256,384},{320,448},{384,256},{4... | collective-permute-start | bytes 1843208 | tf_op jit(solution)/shard_map/ppermute | solution.py:68
  19.0 6.2 %all-to-all-done = f32[8,576,32]{1,2,0:T(8,128)S(1)} async-done(((f32[8,576,32]{1,2,0:T(8,128)}), f32[8,576,32]{1,2,0:T(8,128)S(1)}, u32[]{:S(2)}, u32[]{:S(2)}) %all-to-all-start) | async-done | bytes 589856 | tf_op jit(solution)/shard_map/all_to_all | solution.py:44
  25.2 0.9 broadcast_in_dim.23
  26.1 3.5 %all-to-all-start.1 = ((f32[8,576,32]{1,2,0:T(8,128)}), f32[8,576,32]{1,2,0:T(8,128)S(1)}, u32[]{:S(2)}, u32[]{:S(2)}) async-start(f32[8,576,32]{1,2,0:T(8,128)} %broadcast_in_dim.23), calls=%async_computation.1 | async-start | bytes 1310720 | tf_op jit(solution)/shard_map/all_to_all | solution.py:44
  29.6 8.7 %collective-permute-done = f32[192,800]{1,0:T(8,128)S(1)} collective-permute-done((f32[192,800]{1,0:T(8,128)}, f32[192,800]{1,0:T(8,128)S(1)}, u32[]{:S(2)}, u32[]{:S(2)}) %collective-permute-start) | collective-permute-done | bytes 614432 | tf_op jit(solution)/shard_map/ppermute | solution.py:68
  38.4 0.2 fusion.51
  38.6 4.3 %collective-permute-start.1 = (f32[192,800]{1,0:T(8,128)S(1)}, f32[192,800]{1,0:T(8,128)S(1)}, u32[]{:S(2)}, u32[]{:S(2)}) collective-permute-start(f32[192,800]{1,0:T(8,128)S(1)} %fusion.51), channel_id=1, source_target_pairs={{0,256},{64,320},{128,384},{192,448},{256,0},{320,64},{384,128},{4... | collective-permute-start | bytes 1843208 | tf_op jit(solution)/shard_map/ppermute | solution.py:68
  42.9 15.1 %collective-permute-done.1 = f32[192,800]{1,0:T(8,128)S(1)} collective-permute-done((f32[192,800]{1,0:T(8,128)S(1)}, f32[192,800]{1,0:T(8,128)S(1)}, u32[]{:S(2)}, u32[]{:S(2)}) %collective-permute-start.1) | collective-permute-done | bytes 614432 | tf_op jit(solution)/shard_map/ppermute | solution.py:68
  58.1 3.7 %collective-permute-start.2 = (f32[192,800]{1,0:T(8,128)S(1)}, f32[192,800]{1,0:T(8,128)}, u32[]{:S(2)}, u32[]{:S(2)}) collective-permute-start(f32[192,800]{1,0:T(8,128)S(1)} %add.58), channel_id=1, source_target_pairs={{0,64},{64,0},{128,192},{192,128},{256,320},{320,256},{384,448},{4... | collective-permute-start | bytes 1843208 | tf_op jit(solution)/shard_map/ppermute | solution.py:68
  61.9 0.2 fusion.31
  62.0 0.3 fusion.19
  62.3 1.4 collective-permute-done.2
  63.7 1.2 add.59
  65.0 0.3 fusion.12
  65.5 0.3 fusion.21
  65.9 0.9 broadcast_in_dim.24
  66.9 5.5 %all-to-all-start.2 = ((f32[8,672,32]{1,2,0:T(8,128)}), f32[8,672,32]{1,2,0:T(8,128)S(1)}, u32[]{:S(2)}, u32[]{:S(2)}) async-start(f32[8,672,32]{1,2,0:T(8,128)} %broadcast_in_dim.24), calls=%async_computation.2 | async-start | bytes 1572864 | tf_op jit(solution)/shard_map/all_to_all | solution.py:44
  72.4 23.6 %all-to-all-done.2 = f32[8,672,32]{1,2,0:T(8,128)S(1)} async-done(((f32[8,672,32]{1,2,0:T(8,128)}), f32[8,672,32]{1,2,0:T(8,128)S(1)}, u32[]{:S(2)}, u32[]{:S(2)}) %all-to-all-start.2) | async-done | bytes 688160 | tf_op jit(solution)/shard_map/all_to_all | solution.py:44
  96.4 0.2 fusion.7
  96.7 0.2 fusion.47
  97.1 0.2 fusion.6
  97.6 0.2 fusion.5
  98.4 0.3 convolution_multiply_fusion.1
  98.7 0.2 convolution_multiply_fusion.3
  98.9 0.5 fusion.10
  99.4 0.5 fusion.57
  100.0 25.8 %all_to_all.25 = f32[8,576,32]{1,2,0:T(8,128)S(1)} all-to-all(f32[8,576,32]{1,2,0:T(8,128)S(1)} %broadcast_in_dim.26), channel_id=1, replica_groups=mesh['replica'=8,'shard'=8,'tensor'=8] {'tensor'}, dimensions={0} | all-to-all | bytes 1179648 | tf_op jit(solution)/shard_map/all_to_all | solution.py:44
  125.9 0.3 fusion.8
  126.2 0.3 fusion.27
  126.6 0.3 fusion.25
  127.2 22.7 %all_to_all.26 = f32[8,672,32]{1,2,0:T(8,128)S(1)} all-to-all(f32[8,672,32]{1,2,0:T(8,128)S(1)} %broadcast_in_dim.27), channel_id=1, replica_groups=mesh['replica'=8,'shard'=8,'tensor'=8] {'shard'}, dimensions={0} | all-to-all | bytes 1376256 | tf_op jit(solution)/shard_map/all_to_all | solution.py:44
  150.3 0.2 fusion.3
  150.6 0.2 fusion.48
  151.0 0.2 fusion.2
  152.3 0.2 convolution_multiply_fusion.2
  152.6 0.3 fusion.23
  152.9 0.2 convolution_multiply_fusion
  153.2 0.2 fusion.34
  153.4 1.4 multiply_subtract_fusion.1
  154.8 1.6 %multiply_subtract_fusion = (f32[192,416]{1,0:T(8,128)}, f32[192,416]{1,0:T(8,128)}, f32[1,192,416]{2,1,0:T(8,128)}) fusion(f32[192,416]{1,0:T(8,128)S(1)} %copy-done.1, f32[192,416]{1,0:T(8,128)S(1)} %copy-done.2, f32[192,416]{1,0:T(8,128)S(1)} %add_bitcast_fusion, f32[192,32]{0,1:T(8,128)S(1)} %fusion.34, f32[416,32]{0,1:T(8,128)S(1)} %convolution_multiply_fusion), kind=kOutput, calls=%fused_computation.24 | convolution fusion | flops 31070208 | bytes 1994752 | tf_op jit(solution)/shard_map/dot_general | solution.py:17
  (66 shorter events, 4.7 us)
Async XLA Ops:
  0.6 1.4 copy-start
  0.6 1.1 copy-start.7
  0.7 1.3 copy-start.3
  2.0 0.8 copy-start.9
  4.1 21.1 %all-to-all-start = ((f32[8,576,32]{1,2,0:T(8,128)}), f32[8,576,32]{1,2,0:T(8,128)S(1)}, u32[]{:S(2)}, u32[]{:S(2)}) async-start(f32[8,576,32]{1,2,0:T(8,128)} %broadcast_in_dim.22), calls=%async_computation | async-start | bytes 1310720 | tf_op jit(solution)/shard_map/all_to_all | solution.py:44
  15.7 22.7 %collective-permute-start = (f32[192,800]{1,0:T(8,128)}, f32[192,800]{1,0:T(8,128)S(1)}, u32[]{:S(2)}, u32[]{:S(2)}) collective-permute-start(f32[192,800]{1,0:T(8,128)} %pad_maximum_fusion), channel_id=1, source_target_pairs={{0,128},{64,192},{128,0},{192,64},{256,384},{320,448},{384,256},{4... | collective-permute-start | bytes 1843208 | tf_op jit(solution)/shard_map/ppermute | solution.py:68
  26.1 35.7 %all-to-all-start.1 = ((f32[8,576,32]{1,2,0:T(8,128)}), f32[8,576,32]{1,2,0:T(8,128)S(1)}, u32[]{:S(2)}, u32[]{:S(2)}) async-start(f32[8,576,32]{1,2,0:T(8,128)} %broadcast_in_dim.23), calls=%async_computation.1 | async-start | bytes 1310720 | tf_op jit(solution)/shard_map/all_to_all | solution.py:44
  38.6 19.4 %collective-permute-start.1 = (f32[192,800]{1,0:T(8,128)S(1)}, f32[192,800]{1,0:T(8,128)S(1)}, u32[]{:S(2)}, u32[]{:S(2)}) collective-permute-start(f32[192,800]{1,0:T(8,128)S(1)} %fusion.51), channel_id=1, source_target_pairs={{0,256},{64,320},{128,384},{192,448},{256,0},{320,64},{384,128},{4... | collective-permute-start | bytes 1843208 | tf_op jit(solution)/shard_map/ppermute | solution.py:68
  58.1 5.6 %collective-permute-start.2 = (f32[192,800]{1,0:T(8,128)S(1)}, f32[192,800]{1,0:T(8,128)}, u32[]{:S(2)}, u32[]{:S(2)}) collective-permute-start(f32[192,800]{1,0:T(8,128)S(1)} %add.58), channel_id=1, source_target_pairs={{0,64},{64,0},{128,192},{192,128},{256,320},{320,256},{384,448},{4... | collective-permute-start | bytes 1843208 | tf_op jit(solution)/shard_map/ppermute | solution.py:68
  66.9 29.1 %all-to-all-start.2 = ((f32[8,672,32]{1,2,0:T(8,128)}), f32[8,672,32]{1,2,0:T(8,128)S(1)}, u32[]{:S(2)}, u32[]{:S(2)}) async-start(f32[8,672,32]{1,2,0:T(8,128)} %broadcast_in_dim.24), calls=%async_computation.2 | async-start | bytes 1572864 | tf_op jit(solution)/shard_map/all_to_all | solution.py:44
  152.0 1.4 copy-start.5
  152.2 1.2 copy-start.4
  152.6 0.8 copy-start.8
  153.1 1.7 %copy-start.6 = (f32[416,32]{0,1:T(8,128)}, f32[416,32]{0,1:T(8,128)S(1)}, u32[]{:S(2)}) copy-start(f32[416,32]{0,1:T(8,128)S(1)} %convolution_multiply_fusion) | copy-start | bytes 159748
  153.4 1.4 copy-start.1
  153.4 1.4 copy-start.2

commit v4 on v3

--- a/solution.py
+++ b/solution.py
@@ -45,12 +45,6 @@
     return jnp.sum(copies, axis=0)
 
 
-def all_sum(x, axes):
-    for axis in axes:
-        x = gather_sum(x, axis)
-    return x
-
-
 def finish(merged, orthonormal, query, weight, moment):
     approx = precise_dot(orthonormal, query.T)
     residue = (merged - approx)[None]
@@ -83,6 +77,10 @@
     )
 
 
+def pad_rows(x, height):
+    return jnp.pad(x, ((0, height - x.shape[0]), (0, 0)))
+
+
 def per_device(
     inproj_grads,
     inproj_error,
@@ -104,25 +102,42 @@
     rows = [m.shape[0] for m in merged]
     cols = [m.shape[1] for m in merged]
     rank = inproj_query.shape[1]
-    queries = [inproj_query, outproj_query]
-    for power_round in range(ROUNDS):
-        if power_round == 0:
-            rows_source, row_axes = merged, ("replica", "tensor")
-        else:
-            rows_source, row_axes = total, ("tensor",)
-        partial = jnp.concatenate([precise_dot(m, q) for m, q in zip(rows_source, queries)], axis=0)
-        summed = all_sum(partial, row_axes) / replicas
-        projected = [summed[: rows[0]], summed[rows[0] :]]
-        pieces = [contract_rows(m, p) for m, p in zip(total, projected)]
-        pieces += [precise_dot(p.T, p) for p in projected]
-        column = all_sum(jnp.concatenate(pieces, axis=0), ("shard",))
-        offsets = [0, cols[0], cols[0] + cols[1]]
-        grams = column[offsets[2] :].reshape(2, rank, rank)
-        inverses = inverse_root(grams)
-        orthos = [precise_dot(p, inverses[i]) for i, p in enumerate(projected)]
-        queries = [
-            precise_dot(column[offsets[i] : offsets[i + 1]], inverses[i]) / replicas for i in range(2)
-        ]
+    first_core = lax.axis_index("replica") % 2 == 0
+
+    def pick(for_inproj, for_outproj):
+        return jnp.where(first_core, for_inproj, for_outproj)
+
+    row_pad = max(rows)
+    col_pad = max(cols) + rank
+
+    def column_step(projected):
+        p_in, p_out = projected[: rows[0]], projected[: rows[1]]
+        side_in = jnp.concatenate([contract_rows(total[0], p_in), precise_dot(p_in.T, p_in)], axis=0)
+        side_out = jnp.concatenate([contract_rows(total[1], p_out), precise_dot(p_out.T, p_out)], axis=0)
+        mine = pick(pad_rows(side_in, col_pad), pad_rows(side_out, col_pad))
+        column = gather_sum(mine, "shard")
+        gram = pick(column[cols[0] : cols[0] + rank], column[cols[1] : cols[1] + rank])
+        inverse = inverse_root(gram[None])[0]
+        return precise_dot(projected, inverse), precise_dot(column, inverse) / replicas
+
+    partial = jnp.concatenate([precise_dot(m, q) for m, q in zip(merged, (inproj_query, outproj_query))], axis=0)
+    summed = gather_sum(partial, "replica")
+    mine = pick(pad_rows(summed[: rows[0]], row_pad), pad_rows(summed[rows[0] :], row_pad))
+    projected = gather_sum(mine, "tensor") / replicas
+    ortho, query = column_step(projected)
+    for _ in range(1, ROUNDS):
+        part_in = precise_dot(total[0], query[: cols[0]])
+        part_out = precise_dot(total[1], query[: cols[1]])
+        mine = pick(pad_rows(part_in, row_pad), pad_rows(part_out, row_pad))
+        projected = gather_sum(mine, "tensor") / replicas
+        ortho, query = column_step(projected)
+    held = jnp.concatenate([ortho, query], axis=0)
+    n = lax.axis_size("replica")
+    other = lax.ppermute(held, "replica", [(i, i ^ 1) for i in range(n)])
+    own_in = pick(held, other)
+    own_out = pick(other, held)
+    orthos = [own_in[: rows[0]], own_out[: rows[1]]]
+    queries = [own_in[row_pad : row_pad + cols[0]], own_out[row_pad : row_pad + cols[1]]]
     first = finish(merged[0], orthos[0], queries[0], inproj_weight, inproj_moment)
     second = finish(merged[1], orthos[1], queries[1], outproj_weight, outproj_moment)
     return (first[0], first[1], first[2], first[3], second[0], second[1], second[2], second[3])

time: 159 us -> 144 us (0.906); the launches traced: 156 us -> 143 us
  waiting for transfers between devices: 55 us -> 32.4 us
  blocking collectives: 48.5 us -> 58.1 us
    all_to_all x3 -> x2, waiting for transfers between devices: 29.8 us -> 6.18 us  [gather_sum(): lax.all_to_all(jnp.broadcast_to(x[None], (n,) + x.shape), axis, 0, 0, til...]
    all_to_all x2 -> x3, blocking collectives: 48.5 us -> 58.1 us  [gather_sum(): lax.all_to_all(jnp.broadcast_to(x[None], (n,) + x.shape), axis, 0, 0, til...]
    ppermute x0 -> x1, starting transfers between devices: none -> 6.24 us  [per_device(): other = lax.ppermute(held, 'replica', [(i, i ^ 1) for i in range(n)])]
    all_to_all x3 -> x2, starting transfers between devices: 19.3 us -> 13.7 us  [gather_sum(): lax.all_to_all(jnp.broadcast_to(x[None], (n,) + x.shape), axis, 0, 0, til...]
    dot_general x16 -> x13, matrix products: 7.05 us -> 6.2 us  [precise_dot(): jnp.dot(left, right, precision=lax.Precision.HIGHEST, preferred_element_t...]
where the time goes in v4:
time: 144 us; the launch traced here: 143 us
  blocking collectives  58.1 us (40%)
  waiting for transfers between devices  32.4 us (22%)
  starting transfers between devices  31.3 us (22%)
  matrix products  10.9 us (8%)
  other arithmetic  4.34 us (3%)
  local copies, waits for them, and re-layouts  3.57 us (2%)
  between operations  2.63 us (2%)
    all_to_all x3, blocking collectives, gather_sum(): lax.all_to_all(jnp.broadcast_to(x[None], (n,) + x.shape), axis, 0, 0, til...  58.1 us
    ppermute x3, waiting for transfers between devices, replica_total(): moved = lax.ppermute(flat, 'replica', pairs)  25.3 us
    all_to_all x2, starting transfers between devices, gather_sum(): lax.all_to_all(jnp.broadcast_to(x[None], (n,) + x.shape), axis, 0, 0, til...  13.7 us
    ppermute x3, starting transfers between devices, replica_total(): moved = lax.ppermute(flat, 'replica', pairs)  11.3 us
    ppermute x1, starting transfers between devices, per_device(): other = lax.ppermute(held, 'replica', [(i, i ^ 1) for i in range(n)])  6.24 us
    dot_general x13, matrix products, precise_dot(): jnp.dot(left, right, precision=lax.Precision.HIGHEST, preferred_element_t...  6.2 us
    all_to_all x2, waiting for transfers between devices, gather_sum(): lax.all_to_all(jnp.broadcast_to(x[None], (n,) + x.shape), axis, 0, 0, til...  6.18 us
    dot_general x22, matrix products, batched_dot(): jnp.einsum('bij,bjk->bik', left, right, precision=lax.Precision.HIGHEST,...  3.36 us
  transfers between devices with their start and end apart: 6, of which 5 were waited for; matrix products, arithmetic and copies ran while one was open for 2% of the time, Pallas kernels for 0%

profile of v4, /device:TPU:1, one launch (start us, length us, event | category | flops | bytes accessed | tf_op | source)
XLA Modules:
  0.0 143.2 jit_solution(15338565632226087820)
XLA Ops:
  0.7 1.1 convert_add_fusion
  1.8 0.3 fusion.14
  2.1 0.6 copy-done.7
  2.8 0.5 fusion.48
  3.3 0.9 broadcast_in_dim.14
  4.2 10.3 %all-to-all-start = ((f32[8,576,32]{1,2,0:T(8,128)}), f32[8,576,32]{1,2,0:T(8,128)S(1)}, u32[]{:S(2)}, u32[]{:S(2)}) async-start(f32[8,576,32]{1,2,0:T(8,128)} %broadcast_in_dim.14), calls=%async_computation | async-start | bytes 1310720 | tf_op jit(solution)/shard_map/all_to_all | solution.py:44
  14.5 0.2 copy.31
  14.8 1.0 pad_maximum_fusion
  15.8 3.3 %collective-permute-start = (f32[192,800]{1,0:T(8,128)}, f32[192,800]{1,0:T(8,128)S(1)}, u32[]{:S(2)}, u32[]{:S(2)}) collective-permute-start(f32[192,800]{1,0:T(8,128)} %pad_maximum_fusion), channel_id=1, source_target_pairs={{0,128},{64,192},{128,0},{192,64},{256,384},{320,448},{384,256},{4... | collective-permute-start | bytes 1843208 | tf_op jit(solution)/shard_map/ppermute | solution.py:62
  19.1 6.2 %all-to-all-done = f32[8,576,32]{1,2,0:T(8,128)S(1)} async-done(((f32[8,576,32]{1,2,0:T(8,128)}), f32[8,576,32]{1,2,0:T(8,128)S(1)}, u32[]{:S(2)}, u32[]{:S(2)}) %all-to-all-start) | async-done | bytes 589856 | tf_op jit(solution)/shard_map/all_to_all | solution.py:44
  25.4 0.8 broadcast_in_dim.15
  26.2 3.5 %all-to-all-start.1 = ((f32[8,384,32]{1,2,0:T(8,128)}), f32[8,384,32]{1,2,0:T(8,128)S(1)}, u32[]{:S(2)}, u32[]{:S(2)}) async-start(f32[8,384,32]{1,2,0:T(8,128)} %broadcast_in_dim.15), calls=%async_computation.1 | async-start | bytes 786432 | tf_op jit(solution)/shard_map/all_to_all | solution.py:44
  29.6 8.9 %collective-permute-done = f32[192,800]{1,0:T(8,128)S(1)} collective-permute-done((f32[192,800]{1,0:T(8,128)}, f32[192,800]{1,0:T(8,128)S(1)}, u32[]{:S(2)}, u32[]{:S(2)}) %collective-permute-start) | collective-permute-done | bytes 614432 | tf_op jit(solution)/shard_map/ppermute | solution.py:62
  38.5 0.2 fusion.43
  38.7 4.3 %collective-permute-start.1 = (f32[192,800]{1,0:T(8,128)S(1)}, f32[192,800]{1,0:T(8,128)S(1)}, u32[]{:S(2)}, u32[]{:S(2)}) collective-permute-start(f32[192,800]{1,0:T(8,128)S(1)} %fusion.43), channel_id=1, source_target_pairs={{0,256},{64,320},{128,384},{192,448},{256,0},{320,64},{384,128},{4... | collective-permute-start | bytes 1843208 | tf_op jit(solution)/shard_map/ppermute | solution.py:62
  43.1 15.0 %collective-permute-done.1 = f32[192,800]{1,0:T(8,128)S(1)} collective-permute-done((f32[192,800]{1,0:T(8,128)S(1)}, f32[192,800]{1,0:T(8,128)S(1)}, u32[]{:S(2)}, u32[]{:S(2)}) %collective-permute-start.1) | collective-permute-done | bytes 614432 | tf_op jit(solution)/shard_map/ppermute | solution.py:62
  58.2 3.7 %collective-permute-start.2 = (f32[192,800]{1,0:T(8,128)S(1)}, f32[192,800]{1,0:T(8,128)S(1)}, u32[]{:S(2)}, u32[]{:S(2)}) collective-permute-start(f32[192,800]{1,0:T(8,128)S(1)} %add.55), channel_id=1, source_target_pairs={{0,64},{64,0},{128,192},{192,128},{256,320},{320,256},{384,448},{4... | collective-permute-start | bytes 1843208 | tf_op jit(solution)/shard_map/ppermute | solution.py:62
  61.9 0.2 fusion.31
  62.1 0.2 fusion.38
  62.3 1.4 collective-permute-done.2
  63.7 0.3 fusion.12
  64.4 0.3 fusion.39
  64.8 22.0 %all_to_all.25 = f32[8,448,32]{1,2,0:T(8,128)S(1)} all-to-all(f32[8,448,32]{1,2,0:T(8,128)S(1)} %broadcast_in_dim.16), channel_id=1, replica_groups=mesh['replica'=8,'shard'=8,'tensor'=8] {'shard'}, dimensions={0} | all-to-all | bytes 917504 | tf_op jit(solution)/shard_map/all_to_all | solution.py:44
  86.9 0.7 multiply_reduce_fusion.1
  88.5 0.2 fusion.36
  88.8 0.2 fusion.6
  89.3 0.2 fusion.5
  89.8 0.2 fusion.4
  90.1 0.3 convolution_multiply_fusion.1
  90.3 0.5 fusion.10
  90.8 0.5 pad_select_fusion
  91.3 18.9 %all_to_all.26 = f32[8,384,32]{1,2,0:T(8,128)S(1)} all-to-all(f32[8,384,32]{1,2,0:T(8,128)S(1)} %broadcast_in_dim.17), channel_id=1, replica_groups=mesh['replica'=8,'shard'=8,'tensor'=8] {'tensor'}, dimensions={0} | all-to-all | bytes 786432 | tf_op jit(solution)/shard_map/all_to_all | solution.py:44
  110.2 0.3 fusion.42
  110.6 0.2 fusion.41
  110.8 0.3 fusion.8
  111.1 0.2 fusion.28
  111.5 17.2 %all_to_all.27 = f32[8,448,32]{1,2,0:T(8,128)S(1)} all-to-all(f32[8,448,32]{1,2,0:T(8,128)S(1)} %broadcast_in_dim.18), channel_id=1, replica_groups=mesh['replica'=8,'shard'=8,'tensor'=8] {'shard'}, dimensions={0} | all-to-all | bytes 917504 | tf_op jit(solution)/shard_map/all_to_all | solution.py:44
  128.7 0.7 multiply_reduce_fusion
  130.2 0.2 fusion.37
  131.0 0.2 fusion.1
  131.5 0.2 fusion
  131.8 0.3 convolution_multiply_fusion
  132.1 0.2 fusion.40
  132.4 6.2 %collective-permute-start.3 = (f32[832,32]{0,1:T(8,128)S(1)}, f32[832,32]{0,1:T(8,128)S(1)}, u32[]{:S(2)}, u32[]{:S(2)}) collective-permute-start(f32[832,32]{0,1:T(8,128)S(1)} %pad_maximum_fusion.1), channel_id=1, source_target_pairs={{0,64},{64,0},{128,192},{192,128},{256,320},{320,256},{384,448},{4... | collective-permute-start | bytes 319496 | tf_op jit(solution)/shard_map/ppermute | solution.py:136
  138.6 0.9 collective-permute-done.3
  139.6 0.6 copy-done.8
  140.2 1.4 multiply_subtract_fusion.1
  141.6 1.6 %multiply_subtract_fusion = (f32[192,416]{1,0:T(8,128)}, f32[192,416]{1,0:T(8,128)}, f32[1,192,416]{2,1,0:T(8,128)}) fusion(f32[192,416]{1,0:T(8,128)S(1)} %copy-done.1, f32[192,416]{1,0:T(8,128)S(1)} %copy-done.2, f32[192,416]{1,0:T(8,128)S(1)} %add_bitcast_fusion, f32[416,32]{0,1:T(8,128)S(1)} %slice.78, f32[832,32]{0,1:T(8,128)S(1)} %get-tuple-element.19), kind=kOutput, calls=%fused_computation.22 | convolution fusion | flops 31070208 | bytes 2236416 | tf_op jit(solution)/shard_map/dot_general | solution.py:17
  (60 shorter events, 3.4 us)
Async XLA Ops:
  0.6 2.1 %copy-start = (f32[416,32]{0,1:T(8,128)S(1)}, f32[416,32]{0,1:T(8,128)}, u32[]{:S(2)}) copy-start(f32[416,32]{0,1:T(8,128)} %param.14) | copy-start | bytes 159748
  0.6 1.1 copy-start.9
  0.7 1.5 %copy-start.3 = (f32[1,192,416]{2,1,0:T(8,128)S(1)}, f32[1,192,416]{2,1,0:T(8,128)}, u32[]{:S(2)}) copy-start(f32[1,192,416]{2,1,0:T(8,128)} %param.11) | copy-start | bytes 958468
  1.8 1.0 copy-start.7
  4.2 21.1 %all-to-all-start = ((f32[8,576,32]{1,2,0:T(8,128)}), f32[8,576,32]{1,2,0:T(8,128)S(1)}, u32[]{:S(2)}, u32[]{:S(2)}) async-start(f32[8,576,32]{1,2,0:T(8,128)} %broadcast_in_dim.14), calls=%async_computation | async-start | bytes 1310720 | tf_op jit(solution)/shard_map/all_to_all | solution.py:44
  15.8 22.7 %collective-permute-start = (f32[192,800]{1,0:T(8,128)}, f32[192,800]{1,0:T(8,128)S(1)}, u32[]{:S(2)}, u32[]{:S(2)}) collective-permute-start(f32[192,800]{1,0:T(8,128)} %pad_maximum_fusion), channel_id=1, source_target_pairs={{0,128},{64,192},{128,0},{192,64},{256,384},{320,448},{384,256},{4... | collective-permute-start | bytes 1843208 | tf_op jit(solution)/shard_map/ppermute | solution.py:62
  19.1 6.2 %copy-start.10 = (pred[384]{0:T(512)(128)(4,1)S(1)}, pred[384]{0:T(512)(128)(4,1)}, u32[]{:S(2)}) copy-start(pred[384]{0:T(512)(128)(4,1)} %constant.40.clone.1) | copy-start | bytes 1156
  26.2 16.8 %all-to-all-start.1 = ((f32[8,384,32]{1,2,0:T(8,128)}), f32[8,384,32]{1,2,0:T(8,128)S(1)}, u32[]{:S(2)}, u32[]{:S(2)}) async-start(f32[8,384,32]{1,2,0:T(8,128)} %broadcast_in_dim.15), calls=%async_computation.1 | async-start | bytes 786432 | tf_op jit(solution)/shard_map/all_to_all | solution.py:44
  38.7 19.4 %collective-permute-start.1 = (f32[192,800]{1,0:T(8,128)S(1)}, f32[192,800]{1,0:T(8,128)S(1)}, u32[]{:S(2)}, u32[]{:S(2)}) collective-permute-start(f32[192,800]{1,0:T(8,128)S(1)} %fusion.43), channel_id=1, source_target_pairs={{0,256},{64,320},{128,384},{192,448},{256,0},{320,64},{384,128},{4... | collective-permute-start | bytes 1843208 | tf_op jit(solution)/shard_map/ppermute | solution.py:62
  58.2 5.5 %collective-permute-start.2 = (f32[192,800]{1,0:T(8,128)S(1)}, f32[192,800]{1,0:T(8,128)S(1)}, u32[]{:S(2)}, u32[]{:S(2)}) collective-permute-start(f32[192,800]{1,0:T(8,128)S(1)} %add.55), channel_id=1, source_target_pairs={{0,64},{64,0},{128,192},{192,128},{256,320},{320,256},{384,448},{4... | collective-permute-start | bytes 1843208 | tf_op jit(solution)/shard_map/ppermute | solution.py:62
  132.3 7.9 %copy-start.4 = (f32[384,192]{0,1:T(8,128)S(1)}, f32[384,192]{0,1:T(8,128)}, u32[]{:S(2)}) copy-start(f32[384,192]{0,1:T(8,128)} %param.17) | copy-start | bytes 884740
  132.4 7.9 %copy-start.5 = (f32[384,192]{0,1:T(8,128)S(1)}, f32[384,192]{0,1:T(8,128)}, u32[]{:S(2)}) copy-start(f32[384,192]{0,1:T(8,128)} %param.18) | copy-start | bytes 884740
  132.4 7.2 %collective-permute-start.3 = (f32[832,32]{0,1:T(8,128)S(1)}, f32[832,32]{0,1:T(8,128)S(1)}, u32[]{:S(2)}, u32[]{:S(2)}) collective-permute-start(f32[832,32]{0,1:T(8,128)S(1)} %pad_maximum_fusion.1), channel_id=1, source_target_pairs={{0,64},{64,0},{128,192},{192,128},{256,320},{320,256},{384,448},{4... | collective-permute-start | bytes 319496 | tf_op jit(solution)/shard_map/ppermute | solution.py:136
  139.6 0.6 copy-start.8
  140.2 1.4 copy-start.6
  140.2 1.4 copy-start.1
  140.2 1.4 copy-start.2

commit v5 on v4

--- a/solution.py
+++ b/solution.py
@@ -53,18 +53,18 @@
     return (master, velocity, residue, query)
 
 
-def replica_total(blocks, order):
+def replica_total(blocks, keep_first, order):
     n = lax.axis_size("replica")
-    height = blocks[0].shape[0]
-    flat = jnp.concatenate([b.reshape(height, -1) for b in blocks], axis=1)
+    height, width = blocks[0].shape
+    second = jnp.pad(blocks[1].reshape(height, -1), ((0, 0), (0, width - blocks[1].size // height)))
+    held = jnp.where(keep_first, blocks[0], second)
+    sent = jnp.where(keep_first, second, blocks[0])
     for d in order:
         pairs = [(i, i ^ d) for i in range(n)]
-        moved = lax.ppermute(flat, "replica", pairs)
-        flat = flat + moved
-    widths = [b.size // height for b in blocks]
-    first = flat[:, : widths[0]].reshape(blocks[0].shape)
-    second = flat[:, widths[0] :].reshape(blocks[1].shape)
-    return (first, second)
+        moved = lax.ppermute(sent, "replica", pairs)
+        held = held + moved
+        sent = held
+    return held, held[:, : blocks[1].size // height].reshape(blocks[1].shape)
 
 
 def contract_rows(m, p):
@@ -98,11 +98,11 @@
         inproj_grads[0].astype(jnp.float32) + inproj_error[0],
         outproj_grads[0].astype(jnp.float32) + outproj_error[0],
     )
-    total = replica_total(merged, (2, 4, 1))
     rows = [m.shape[0] for m in merged]
     cols = [m.shape[1] for m in merged]
     rank = inproj_query.shape[1]
     first_core = lax.axis_index("replica") % 2 == 0
+    total = replica_total(merged, first_core, (1, 2, 4))
 
     def pick(for_inproj, for_outproj):
         return jnp.where(first_core, for_inproj, for_outproj)

time: 144 us -> 132 us (0.917)
  waiting for transfers between devices: 32.4 us -> 28.2 us
  blocking collectives: 58.1 us -> 54.8 us
  starting transfers between devices: 31.3 us -> 28.8 us
    ppermute x3, waiting for transfers between devices: 25.3 us -> 18.8 us  [replica_total(): moved = lax.ppermute(sent, 'replica', pairs)]
    ppermute x3, starting transfers between devices: 11.3 us -> 7.01 us  [replica_total(): moved = lax.ppermute(sent, 'replica', pairs)]
    all_to_all x3, blocking collectives: 58.1 us -> 54.8 us  [gather_sum(): lax.all_to_all(jnp.broadcast_to(x[None], (n,) + x.shape), axis, 0, 0, til...]
    all_to_all x2, waiting for transfers between devices: 6.18 us -> 8.37 us  [gather_sum(): lax.all_to_all(jnp.broadcast_to(x[None], (n,) + x.shape), axis, 0, 0, til...]
    ppermute x1, starting transfers between devices: 6.24 us -> 8.08 us  [per_device(): other = lax.ppermute(held, 'replica', [(i, i ^ 1) for i in range(n)])]
  transfers between devices with their start and end apart: 6 -> 6, of which waited for: 5 -> 4; matrix products, arithmetic and copies ran while one was open for 2% -> 1% of each run, Pallas kernels for 0% -> 0%
where the time goes in v5:
time: 132 us
  blocking collectives  54.8 us (42%)
  starting transfers between devices  28.8 us (22%)
  waiting for transfers between devices  28.2 us (21%)
  matrix products  10.9 us (8%)
  other arithmetic  3.24 us (2%)
  local copies, waits for them, and re-layouts  2.87 us (2%)
  between operations  2.73 us (2%)
    all_to_all x3, blocking collectives, gather_sum(): lax.all_to_all(jnp.broadcast_to(x[None], (n,) + x.shape), axis, 0, 0, til...  54.8 us
    ppermute x3, waiting for transfers between devices, replica_total(): moved = lax.ppermute(sent, 'replica', pairs)  18.8 us
    all_to_all x2, starting transfers between devices, gather_sum(): lax.all_to_all(jnp.broadcast_to(x[None], (n,) + x.shape), axis, 0, 0, til...  13.7 us
    all_to_all x2, waiting for transfers between devices, gather_sum(): lax.all_to_all(jnp.broadcast_to(x[None], (n,) + x.shape), axis, 0, 0, til...  8.37 us
    ppermute x1, starting transfers between devices, per_device(): other = lax.ppermute(held, 'replica', [(i, i ^ 1) for i in range(n)])  8.08 us
    ppermute x3, starting transfers between devices, replica_total(): moved = lax.ppermute(sent, 'replica', pairs)  7.01 us
    dot_general x13, matrix products, precise_dot(): jnp.dot(left, right, precision=lax.Precision.HIGHEST, preferred_element_t...  6.23 us
    dot_general x22, matrix products, batched_dot(): jnp.einsum('bij,bjk->bik', left, right, precision=lax.Precision.HIGHEST,...  3.31 us
  transfers between devices with their start and end apart: 6, of which 4 were waited for; matrix products, arithmetic and copies ran while one was open for 1% of the time, Pallas kernels for 0%

profile of v5, /device:TPU:1, one launch (start us, length us, event | category | flops | bytes accessed | tf_op | source)
XLA Modules:
  0.0 131.5 jit_solution(5012973735831051191)
XLA Ops:
  0.7 1.1 convert_add_fusion.1
  1.8 0.3 fusion.12
  2.1 0.6 copy-done.2
  2.7 0.5 fusion.9
  3.3 0.9 broadcast_in_dim.14
  4.1 10.3 %all-to-all-start = ((f32[8,576,32]{1,2,0:T(8,128)}), f32[8,576,32]{1,2,0:T(8,128)S(1)}, u32[]{:S(2)}, u32[]{:S(2)}) async-start(f32[8,576,32]{1,2,0:T(8,128)} %broadcast_in_dim.14), calls=%async_computation | async-start | bytes 1310720 | tf_op jit(solution)/shard_map/all_to_all | solution.py:44
  14.4 0.2 copy.31
  14.8 2.0 %collective-permute-start = (f32[192,416]{1,0:T(8,128)S(1)}, f32[192,416]{1,0:T(8,128)S(1)}, u32[]{:S(2)}, u32[]{:S(2)}) collective-permute-start(f32[192,416]{1,0:T(8,128)S(1)} %pad_select_fusion), channel_id=1, source_target_pairs={{0,64},{64,0},{128,192},{192,128},{256,320},{320,256},{384,448},{4... | collective-permute-start | bytes 958472 | tf_op jit(solution)/shard_map/ppermute | solution.py:64
  16.8 8.4 %all-to-all-done = f32[8,576,32]{1,2,0:T(8,128)S(1)} async-done(((f32[8,576,32]{1,2,0:T(8,128)}), f32[8,576,32]{1,2,0:T(8,128)S(1)}, u32[]{:S(2)}, u32[]{:S(2)}) %all-to-all-start) | async-done | bytes 589856 | tf_op jit(solution)/shard_map/all_to_all | solution.py:44
  25.3 0.8 broadcast_in_dim.15
  26.1 3.5 %all-to-all-start.1 = ((f32[8,384,32]{1,2,0:T(8,128)}), f32[8,384,32]{1,2,0:T(8,128)S(1)}, u32[]{:S(2)}, u32[]{:S(2)}) async-start(f32[8,384,32]{1,2,0:T(8,128)} %broadcast_in_dim.15), calls=%async_computation.1 | async-start | bytes 786432 | tf_op jit(solution)/shard_map/all_to_all | solution.py:44
  29.7 2.2 %collective-permute-start.1 = (f32[192,416]{1,0:T(8,128)S(1)}, f32[192,416]{1,0:T(8,128)S(1)}, u32[]{:S(2)}, u32[]{:S(2)}) collective-permute-start(f32[192,416]{1,0:T(8,128)S(1)} %fusion.8), channel_id=1, source_target_pairs={{0,128},{64,192},{128,0},{192,64},{256,384},{320,448},{384,256},{4... | collective-permute-start | bytes 958472 | tf_op jit(solution)/shard_map/ppermute | solution.py:64
  31.9 9.4 %collective-permute-done.1 = f32[192,416]{1,0:T(8,128)S(1)} collective-permute-done((f32[192,416]{1,0:T(8,128)S(1)}, f32[192,416]{1,0:T(8,128)S(1)}, u32[]{:S(2)}, u32[]{:S(2)}) %collective-permute-start.1) | collective-permute-done | bytes 319520 | tf_op jit(solution)/shard_map/ppermute | solution.py:64
  41.4 2.8 %collective-permute-start.2 = (f32[192,416]{1,0:T(8,128)S(1)}, f32[192,416]{1,0:T(8,128)S(1)}, u32[]{:S(2)}, u32[]{:S(2)}) collective-permute-start(f32[192,416]{1,0:T(8,128)S(1)} %add.57), channel_id=1, source_target_pairs={{0,256},{64,320},{128,384},{192,448},{256,0},{320,64},{384,128},{4... | collective-permute-start | bytes 958472 | tf_op jit(solution)/shard_map/ppermute | solution.py:64
  44.2 9.5 %collective-permute-done.2 = f32[192,416]{1,0:T(8,128)S(1)} collective-permute-done((f32[192,416]{1,0:T(8,128)S(1)}, f32[192,416]{1,0:T(8,128)S(1)}, u32[]{:S(2)}, u32[]{:S(2)}) %collective-permute-start.2) | collective-permute-done | bytes 319520 | tf_op jit(solution)/shard_map/ppermute | solution.py:64
  53.9 0.2 fusion.39
  54.1 0.2 fusion.31
  54.3 0.3 fusion.33
  54.6 0.3 fusion.40
  55.1 21.6 %all_to_all.25 = f32[8,448,32]{1,2,0:T(8,128)S(1)} all-to-all(f32[8,448,32]{1,2,0:T(8,128)S(1)} %broadcast_in_dim.16), channel_id=1, replica_groups=mesh['replica'=8,'shard'=8,'tensor'=8] {'shard'}, dimensions={0} | all-to-all | bytes 917504 | tf_op jit(solution)/shard_map/all_to_all | solution.py:44
  76.7 0.7 multiply_reduce_fusion.1
  78.4 0.2 fusion.37
  78.6 0.1 fusion.6
  78.9 0.1 fusion.49
  79.0 0.2 fusion.5
  79.3 0.1 fusion.51
  79.7 0.1 convolution_divide_fusion.1
  79.9 0.3 convolution_multiply_fusion.1
  80.1 0.5 fusion.16
  80.6 0.5 pad_select_fusion.2
  81.1 16.3 %all_to_all.26 = f32[8,384,32]{1,2,0:T(8,128)S(1)} all-to-all(f32[8,384,32]{1,2,0:T(8,128)S(1)} %broadcast_in_dim.17), channel_id=1, replica_groups=mesh['replica'=8,'shard'=8,'tensor'=8] {'tensor'}, dimensions={0} | all-to-all | bytes 786432 | tf_op jit(solution)/shard_map/all_to_all | solution.py:44
  97.5 0.2 fusion.42
  97.7 0.3 fusion.43
  98.0 0.2 fusion.27
  98.2 0.3 fusion.29
  98.7 16.9 %all_to_all.27 = f32[8,448,32]{1,2,0:T(8,128)S(1)} all-to-all(f32[8,448,32]{1,2,0:T(8,128)S(1)} %broadcast_in_dim.18), channel_id=1, replica_groups=mesh['replica'=8,'shard'=8,'tensor'=8] {'shard'}, dimensions={0} | all-to-all | bytes 917504 | tf_op jit(solution)/shard_map/all_to_all | solution.py:44
  115.7 0.7 multiply_reduce_fusion
  117.3 0.2 fusion.38
  117.8 0.1 fusion.53
  118.0 0.2 fusion.1
  118.3 0.1 fusion.55
  118.7 0.1 convolution_divide_fusion
  118.8 0.3 convolution_multiply_fusion
  119.1 0.2 fusion.41
  119.4 8.1 %collective-permute-start.3 = (f32[832,32]{0,1:T(8,128)S(1)}, f32[832,32]{0,1:T(8,128)S(1)}, u32[]{:S(2)}, u32[]{:S(2)}) collective-permute-start(f32[832,32]{0,1:T(8,128)S(1)} %pad_maximum_fusion), channel_id=1, source_target_pairs={{0,64},{64,0},{128,192},{192,128},{256,320},{320,256},{384,448},{4... | collective-permute-start | bytes 319496 | tf_op jit(solution)/shard_map/ppermute | solution.py:136
  127.5 0.9 collective-permute-done.3
  128.5 1.6 %multiply_subtract_fusion = (f32[192,416]{1,0:T(8,128)}, f32[192,416]{1,0:T(8,128)}, f32[1,192,416]{2,1,0:T(8,128)}) fusion(f32[192,416]{1,0:T(8,128)S(1)} %copy-done.3, f32[192,416]{1,0:T(8,128)S(1)} %copy-done.4, f32[1,192,416]{2,1,0:T(8,128)S(1)} %copy-done.1, bf16[1,192,416]{2,1,0:T(8,128)(2,1)S(1)} %copy-done.2, f32[416,32]{0,1:T(8,128)S(1)} %slice.73, ...), kind=kOutput, calls=%fused_computation.27 | convolution fusion | flops 31229952 | bytes 2433024 | tf_op jit(solution)/shard_map/dot_general | solution.py:17
  130.2 1.4 %multiply_subtract_fusion.1 = (f32[384,192]{0,1:T(8,128)}, f32[384,192]{0,1:T(8,128)}, f32[1,384,192]{1,2,0:T(8,128)}) fusion(f32[384,192]{0,1:T(8,128)S(1)} %copy-done.5, f32[384,192]{0,1:T(8,128)S(1)} %copy-done.6, f32[1,384,192]{1,2,0:T(8,128)S(1)} %convert_add_fusion.1, f32[192,32]{0,1:T(8,128)S(1)} %slice.75, f32[832,32]{0,1:T(8,128)S(1)} %get-tuple-element.18), kind=kOutput, calls=%fused_computation.34 | convolution fusion | flops 28680192 | bytes 1851392 | tf_op jit(solution)/shard_map/dot_general | solution.py:17
  (59 shorter events, 2.8 us)
Async XLA Ops:
  0.6 1.5 %copy-start = (f32[416,32]{0,1:T(8,128)S(1)}, f32[416,32]{0,1:T(8,128)}, u32[]{:S(2)}) copy-start(f32[416,32]{0,1:T(8,128)} %param.14) | copy-start | bytes 159748
  0.6 1.1 copy-start.9
  0.7 1.5 %copy-start.1 = (f32[1,192,416]{2,1,0:T(8,128)S(1)}, f32[1,192,416]{2,1,0:T(8,128)}, u32[]{:S(2)}) copy-start(f32[1,192,416]{2,1,0:T(8,128)} %param.11) | copy-start | bytes 958468
  1.8 1.0 copy-start.2
  4.1 21.1 %all-to-all-start = ((f32[8,576,32]{1,2,0:T(8,128)}), f32[8,576,32]{1,2,0:T(8,128)S(1)}, u32[]{:S(2)}, u32[]{:S(2)}) async-start(f32[8,576,32]{1,2,0:T(8,128)} %broadcast_in_dim.14), calls=%async_computation | async-start | bytes 1310720 | tf_op jit(solution)/shard_map/all_to_all | solution.py:44
  14.8 10.4 %copy-start.10 = (pred[384]{0:T(512)(128)(4,1)S(1)}, pred[384]{0:T(512)(128)(4,1)}, u32[]{:S(2)}) copy-start(pred[384]{0:T(512)(128)(4,1)} %constant.41.clone.1) | copy-start | bytes 1156
  14.8 14.8 %collective-permute-start = (f32[192,416]{1,0:T(8,128)S(1)}, f32[192,416]{1,0:T(8,128)S(1)}, u32[]{:S(2)}, u32[]{:S(2)}) collective-permute-start(f32[192,416]{1,0:T(8,128)S(1)} %pad_select_fusion), channel_id=1, source_target_pairs={{0,64},{64,0},{128,192},{192,128},{256,320},{320,256},{384,448},{4... | collective-permute-start | bytes 958472 | tf_op jit(solution)/shard_map/ppermute | solution.py:64
  26.1 27.7 %all-to-all-start.1 = ((f32[8,384,32]{1,2,0:T(8,128)}), f32[8,384,32]{1,2,0:T(8,128)S(1)}, u32[]{:S(2)}, u32[]{:S(2)}) async-start(f32[8,384,32]{1,2,0:T(8,128)} %broadcast_in_dim.15), calls=%async_computation.1 | async-start | bytes 786432 | tf_op jit(solution)/shard_map/all_to_all | solution.py:44
  29.7 11.6 %collective-permute-start.1 = (f32[192,416]{1,0:T(8,128)S(1)}, f32[192,416]{1,0:T(8,128)S(1)}, u32[]{:S(2)}, u32[]{:S(2)}) collective-permute-start(f32[192,416]{1,0:T(8,128)S(1)} %fusion.8), channel_id=1, source_target_pairs={{0,128},{64,192},{128,0},{192,64},{256,384},{320,448},{384,256},{4... | collective-permute-start | bytes 958472 | tf_op jit(solution)/shard_map/ppermute | solution.py:64
  41.4 12.3 %collective-permute-start.2 = (f32[192,416]{1,0:T(8,128)S(1)}, f32[192,416]{1,0:T(8,128)S(1)}, u32[]{:S(2)}, u32[]{:S(2)}) collective-permute-start(f32[192,416]{1,0:T(8,128)S(1)} %add.57), channel_id=1, source_target_pairs={{0,256},{64,320},{128,384},{192,448},{256,0},{320,64},{384,128},{4... | collective-permute-start | bytes 958472 | tf_op jit(solution)/shard_map/ppermute | solution.py:64
  119.3 9.1 %copy-start.3 = (f32[192,416]{1,0:T(8,128)S(1)}, f32[192,416]{1,0:T(8,128)}, u32[]{:S(2)}) copy-start(f32[192,416]{1,0:T(8,128)} %param.12) | copy-start | bytes 958468
  119.3 9.1 %copy-start.4 = (f32[192,416]{1,0:T(8,128)S(1)}, f32[192,416]{1,0:T(8,128)}, u32[]{:S(2)}) copy-start(f32[192,416]{1,0:T(8,128)} %param.13) | copy-start | bytes 958468
  119.4 9.0 %collective-permute-start.3 = (f32[832,32]{0,1:T(8,128)S(1)}, f32[832,32]{0,1:T(8,128)S(1)}, u32[]{:S(2)}, u32[]{:S(2)}) collective-permute-start(f32[832,32]{0,1:T(8,128)S(1)} %pad_maximum_fusion), channel_id=1, source_target_pairs={{0,64},{64,0},{128,192},{192,128},{256,320},{320,256},{384,448},{4... | collective-permute-start | bytes 319496 | tf_op jit(solution)/shard_map/ppermute | solution.py:136
  128.4 1.7 %copy-start.7 = (f32[416,32]{0,1:T(8,128)}, f32[416,32]{0,1:T(8,128)S(1)}, u32[]{:S(2)}) copy-start(f32[416,32]{0,1:T(8,128)S(1)} %slice.73) | copy-start | bytes 159748
  128.5 1.7 %copy-start.8 = (f32[192,32]{0,1:T(8,128)}, f32[192,32]{0,1:T(8,128)S(1)}, u32[]{:S(2)}) copy-start(f32[192,32]{0,1:T(8,128)S(1)} %slice.75) | copy-start | bytes 73732
  128.5 1.7 %copy-start.5 = (f32[384,192]{0,1:T(8,128)S(1)}, f32[384,192]{0,1:T(8,128)}, u32[]{:S(2)}) copy-start(f32[384,192]{0,1:T(8,128)} %param.17) | copy-start | bytes 884740
  128.5 1.6 %copy-start.6 = (f32[384,192]{0,1:T(8,128)S(1)}, f32[384,192]{0,1:T(8,128)}, u32[]{:S(2)}) copy-start(f32[384,192]{0,1:T(8,128)} %param.18) | copy-start | bytes 884740

commit v6 on v5

--- a/solution.py
+++ b/solution.py
@@ -59,10 +59,12 @@
     second = jnp.pad(blocks[1].reshape(height, -1), ((0, 0), (0, width - blocks[1].size // height)))
     held = jnp.where(keep_first, blocks[0], second)
     sent = jnp.where(keep_first, second, blocks[0])
-    for d in order:
-        pairs = [(i, i ^ d) for i in range(n)]
-        moved = lax.ppermute(sent, "replica", pairs)
-        held = held + moved
+    for group in order:
+        moved = [lax.ppermute(sent, "replica", [(i, i ^ d) for i in range(n)]) for d in group]
+        if len(moved) == 1:
+            held = held + moved[0]
+        else:
+            held = (held + moved[0]) + (moved[1] + moved[2])
         sent = held
     return held, held[:, : blocks[1].size // height].reshape(blocks[1].shape)
 
@@ -102,7 +104,7 @@
     cols = [m.shape[1] for m in merged]
     rank = inproj_query.shape[1]
     first_core = lax.axis_index("replica") % 2 == 0
-    total = replica_total(merged, first_core, (1, 2, 4))
+    total = replica_total(merged, first_core, ((1,), (2, 4, 6)))
 
     def pick(for_inproj, for_outproj):
         return jnp.where(first_core, for_inproj, for_outproj)

time: 132 us -> 136 us (1.030)
  blocking collectives: 54.8 us -> 61.5 us
  waiting for transfers between devices: 28.2 us -> 23.7 us
  starting transfers between devices: 28.8 us -> 30.2 us
    all_to_all x3, blocking collectives: 54.8 us -> 61.5 us  [gather_sum(): lax.all_to_all(jnp.broadcast_to(x[None], (n,) + x.shape), axis, 0, 0, til...]
    ppermute x3 -> x4, waiting for transfers between devices: 18.8 us -> 14.4 us  [replica_total(): lax.ppermute(sent, 'replica', [(i, i ^ d) for i in range(n)])]
    ppermute x3 -> x4, starting transfers between devices: 7.01 us -> 10.4 us  [replica_total(): lax.ppermute(sent, 'replica', [(i, i ^ d) for i in range(n)])]
    ppermute x1, starting transfers between devices: 8.08 us -> 5.98 us  [per_device(): other = lax.ppermute(held, 'replica', [(i, i ^ 1) for i in range(n)])]
  transfers between devices with their start and end apart: 6 -> 7, of which waited for: 4 -> 4; matrix products, arithmetic and copies ran while one was open for 1% -> 1% of each run, Pallas kernels for 0% -> 0%
where the time goes in v6:
time: 136 us; the launch traced here: 135 us
  blocking collectives  61.5 us (45%)
  starting transfers between devices  30.2 us (22%)
  waiting for transfers between devices  23.7 us (17%)
  matrix products  10.9 us (8%)
  other arithmetic  3.28 us (2%)
  local copies, waits for them, and re-layouts  2.88 us (2%)
  between operations  2.74 us (2%)
    all_to_all x3, blocking collectives, gather_sum(): lax.all_to_all(jnp.broadcast_to(x[None], (n,) + x.shape), axis, 0, 0, til...  61.5 us
    ppermute x4, waiting for transfers between devices, replica_total(): lax.ppermute(sent, 'replica', [(i, i ^ d) for i in range(n)])  14.4 us
    all_to_all x2, starting transfers between devices, gather_sum(): lax.all_to_all(jnp.broadcast_to(x[None], (n,) + x.shape), axis, 0, 0, til...  13.7 us
    ppermute x4, starting transfers between devices, replica_total(): lax.ppermute(sent, 'replica', [(i, i ^ d) for i in range(n)])  10.4 us
    all_to_all x2, waiting for transfers between devices, gather_sum(): lax.all_to_all(jnp.broadcast_to(x[None], (n,) + x.shape), axis, 0, 0, til...  8.37 us
    dot_general x13, matrix products, precise_dot(): jnp.dot(left, right, precision=lax.Precision.HIGHEST, preferred_element_t...  6.23 us
    ppermute x1, starting transfers between devices, per_device(): other = lax.ppermute(held, 'replica', [(i, i ^ 1) for i in range(n)])  5.98 us
    dot_general x22, matrix products, batched_dot(): jnp.einsum('bij,bjk->bik', left, right, precision=lax.Precision.HIGHEST,...  3.31 us
  transfers between devices with their start and end apart: 7, of which 4 were waited for; matrix products, arithmetic and copies ran while one was open for 1% of the time, Pallas kernels for 0%

profile of v6, /device:TPU:1, one launch (start us, length us, event | category | flops | bytes accessed | tf_op | source)
XLA Modules:
  0.0 135.2 jit_solution(13143793591018085318)
XLA Ops:
  0.7 1.1 convert_add_fusion.1
  1.8 0.3 fusion.12
  2.1 0.6 copy-done.2
  2.7 0.5 fusion.9
  3.3 0.9 broadcast_in_dim.14
  4.2 10.3 %all-to-all-start = ((f32[8,576,32]{1,2,0:T(8,128)}), f32[8,576,32]{1,2,0:T(8,128)S(1)}, u32[]{:S(2)}, u32[]{:S(2)}) async-start(f32[8,576,32]{1,2,0:T(8,128)} %broadcast_in_dim.14), calls=%async_computation | async-start | bytes 1310720 | tf_op jit(solution)/shard_map/all_to_all | solution.py:44
  14.4 0.2 copy.31
  14.8 2.0 %collective-permute-start = (f32[192,416]{1,0:T(8,128)S(1)}, f32[192,416]{1,0:T(8,128)S(1)}, u32[]{:S(2)}, u32[]{:S(2)}) collective-permute-start(f32[192,416]{1,0:T(8,128)S(1)} %pad_select_fusion), channel_id=1, source_target_pairs={{0,64},{64,0},{128,192},{192,128},{256,320},{320,256},{384,448},{4... | collective-permute-start | bytes 958472 | tf_op jit(solution)/shard_map/ppermute | solution.py:63
  16.9 8.4 %all-to-all-done = f32[8,576,32]{1,2,0:T(8,128)S(1)} async-done(((f32[8,576,32]{1,2,0:T(8,128)}), f32[8,576,32]{1,2,0:T(8,128)S(1)}, u32[]{:S(2)}, u32[]{:S(2)}) %all-to-all-start) | async-done | bytes 589856 | tf_op jit(solution)/shard_map/all_to_all | solution.py:44
  25.4 0.8 broadcast_in_dim.15
  26.1 3.5 %all-to-all-start.1 = ((f32[8,384,32]{1,2,0:T(8,128)}), f32[8,384,32]{1,2,0:T(8,128)S(1)}, u32[]{:S(2)}, u32[]{:S(2)}) async-start(f32[8,384,32]{1,2,0:T(8,128)} %broadcast_in_dim.15), calls=%async_computation.1 | async-start | bytes 786432 | tf_op jit(solution)/shard_map/all_to_all | solution.py:44
  29.7 2.3 %collective-permute-start.2 = (f32[192,416]{1,0:T(8,128)S(1)}, f32[192,416]{1,0:T(8,128)S(1)}, u32[]{:S(2)}, u32[]{:S(2)}) collective-permute-start(f32[192,416]{1,0:T(8,128)S(1)} %fusion.8), channel_id=1, source_target_pairs={{0,256},{64,320},{128,384},{192,448},{256,0},{320,64},{384,128},{4... | collective-permute-start | bytes 958472 | tf_op jit(solution)/shard_map/ppermute | solution.py:63
  32.0 4.2 %collective-permute-start.3 = (f32[192,416]{1,0:T(8,128)S(1)}, f32[192,416]{1,0:T(8,128)S(1)}, u32[]{:S(2)}, u32[]{:S(2)}) collective-permute-start(f32[192,416]{1,0:T(8,128)S(1)} %fusion.8), channel_id=1, source_target_pairs={{0,384},{64,448},{128,256},{192,320},{256,128},{320,192},{384,0},{... | collective-permute-start | bytes 958472 | tf_op jit(solution)/shard_map/ppermute | solution.py:63
  36.2 1.9 %collective-permute-start.1 = (f32[192,416]{1,0:T(8,128)S(1)}, f32[192,416]{1,0:T(8,128)S(1)}, u32[]{:S(2)}, u32[]{:S(2)}) collective-permute-start(f32[192,416]{1,0:T(8,128)S(1)} %fusion.8), channel_id=1, source_target_pairs={{0,128},{64,192},{128,0},{192,64},{256,384},{320,448},{384,256},{4... | collective-permute-start | bytes 958472 | tf_op jit(solution)/shard_map/ppermute | solution.py:63
  38.2 4.7 %collective-permute-done.2 = f32[192,416]{1,0:T(8,128)S(1)} collective-permute-done((f32[192,416]{1,0:T(8,128)S(1)}, f32[192,416]{1,0:T(8,128)S(1)}, u32[]{:S(2)}, u32[]{:S(2)}) %collective-permute-start.2) | collective-permute-done | bytes 319520 | tf_op jit(solution)/shard_map/ppermute | solution.py:63
  42.9 9.7 %collective-permute-done.3 = f32[192,416]{1,0:T(8,128)S(1)} collective-permute-done((f32[192,416]{1,0:T(8,128)S(1)}, f32[192,416]{1,0:T(8,128)S(1)}, u32[]{:S(2)}, u32[]{:S(2)}) %collective-permute-start.3) | collective-permute-done | bytes 319520 | tf_op jit(solution)/shard_map/ppermute | solution.py:63
  52.6 0.1 add_add_fusion
  52.9 0.2 fusion.39
  53.1 0.2 fusion.31
  53.3 0.3 fusion.33
  53.7 0.3 fusion.40
  54.2 25.0 %all_to_all.25 = f32[8,448,32]{1,2,0:T(8,128)S(1)} all-to-all(f32[8,448,32]{1,2,0:T(8,128)S(1)} %broadcast_in_dim.16), channel_id=1, replica_groups=mesh['replica'=8,'shard'=8,'tensor'=8] {'shard'}, dimensions={0} | all-to-all | bytes 917504 | tf_op jit(solution)/shard_map/all_to_all | solution.py:44
  79.2 0.7 multiply_reduce_fusion.1
  80.9 0.2 fusion.37
  81.4 0.1 fusion.49
  81.5 0.2 fusion.5
  81.9 0.1 fusion.51
  82.2 0.1 convolution_divide_fusion.1
  82.4 0.3 convolution_multiply_fusion.1
  82.6 0.5 fusion.16
  83.1 0.5 pad_select_fusion.2
  83.7 18.1 %all_to_all.26 = f32[8,384,32]{1,2,0:T(8,128)S(1)} all-to-all(f32[8,384,32]{1,2,0:T(8,128)S(1)} %broadcast_in_dim.17), channel_id=1, replica_groups=mesh['replica'=8,'shard'=8,'tensor'=8] {'tensor'}, dimensions={0} | all-to-all | bytes 786432 | tf_op jit(solution)/shard_map/all_to_all | solution.py:44
  101.7 0.2 fusion.42
  101.9 0.3 fusion.43
  102.3 0.2 fusion.27
  102.5 0.3 fusion.29
  103.0 18.4 %all_to_all.27 = f32[8,448,32]{1,2,0:T(8,128)S(1)} all-to-all(f32[8,448,32]{1,2,0:T(8,128)S(1)} %broadcast_in_dim.18), channel_id=1, replica_groups=mesh['replica'=8,'shard'=8,'tensor'=8] {'shard'}, dimensions={0} | all-to-all | bytes 917504 | tf_op jit(solution)/shard_map/all_to_all | solution.py:44
  121.4 0.7 multiply_reduce_fusion
  123.0 0.2 fusion.38
  123.6 0.1 fusion.53
  123.7 0.2 fusion.1
  124.0 0.1 fusion.55
  124.5 0.3 convolution_multiply_fusion
  124.8 0.2 fusion.41
  125.1 6.0 %collective-permute-start.4 = (f32[832,32]{0,1:T(8,128)S(1)}, f32[832,32]{0,1:T(8,128)S(1)}, u32[]{:S(2)}, u32[]{:S(2)}) collective-permute-start(f32[832,32]{0,1:T(8,128)S(1)} %pad_maximum_fusion), channel_id=1, source_target_pairs={{0,64},{64,0},{128,192},{192,128},{256,320},{320,256},{384,448},{4... | collective-permute-start | bytes 319496 | tf_op jit(solution)/shard_map/ppermute | solution.py:138
  131.1 0.9 collective-permute-done.4
  132.1 1.6 %multiply_subtract_fusion = (f32[192,416]{1,0:T(8,128)}, f32[192,416]{1,0:T(8,128)}, f32[1,192,416]{2,1,0:T(8,128)}) fusion(f32[192,416]{1,0:T(8,128)S(1)} %copy-done.3, f32[192,416]{1,0:T(8,128)S(1)} %copy-done.4, f32[1,192,416]{2,1,0:T(8,128)S(1)} %copy-done.1, bf16[1,192,416]{2,1,0:T(8,128)(2,1)S(1)} %copy-done.2, f32[416,32]{0,1:T(8,128)S(1)} %slice.73, ...), kind=kOutput, calls=%fused_computation.27 | convolution fusion | flops 31229952 | bytes 2433024 | tf_op jit(solution)/shard_map/dot_general | solution.py:17
  133.8 1.4 %multiply_subtract_fusion.1 = (f32[384,192]{0,1:T(8,128)}, f32[384,192]{0,1:T(8,128)}, f32[1,384,192]{1,2,0:T(8,128)}) fusion(f32[384,192]{0,1:T(8,128)S(1)} %copy-done.5, f32[384,192]{0,1:T(8,128)S(1)} %copy-done.6, f32[1,384,192]{1,2,0:T(8,128)S(1)} %convert_add_fusion.1, f32[192,32]{0,1:T(8,128)S(1)} %slice.75, f32[832,32]{0,1:T(8,128)S(1)} %get-tuple-element.18), kind=kOutput, calls=%fused_computation.35 | convolution fusion | flops 28680192 | bytes 1851392 | tf_op jit(solution)/shard_map/dot_general | solution.py:17
  (60 shorter events, 3.0 us)
Async XLA Ops:
  0.6 1.5 %copy-start = (f32[416,32]{0,1:T(8,128)S(1)}, f32[416,32]{0,1:T(8,128)}, u32[]{:S(2)}) copy-start(f32[416,32]{0,1:T(8,128)} %param.14) | copy-start | bytes 159748
  0.6 1.1 copy-start.9
  0.7 1.5 %copy-start.1 = (f32[1,192,416]{2,1,0:T(8,128)S(1)}, f32[1,192,416]{2,1,0:T(8,128)}, u32[]{:S(2)}) copy-start(f32[1,192,416]{2,1,0:T(8,128)} %param.11) | copy-start | bytes 958468
  1.8 1.0 copy-start.2
  4.2 21.1 %all-to-all-start = ((f32[8,576,32]{1,2,0:T(8,128)}), f32[8,576,32]{1,2,0:T(8,128)S(1)}, u32[]{:S(2)}, u32[]{:S(2)}) async-start(f32[8,576,32]{1,2,0:T(8,128)} %broadcast_in_dim.14), calls=%async_computation | async-start | bytes 1310720 | tf_op jit(solution)/shard_map/all_to_all | solution.py:44
  14.8 10.4 %copy-start.10 = (pred[384]{0:T(512)(128)(4,1)S(1)}, pred[384]{0:T(512)(128)(4,1)}, u32[]{:S(2)}) copy-start(pred[384]{0:T(512)(128)(4,1)} %constant.41.clone.1) | copy-start | bytes 1156
  14.8 14.8 %collective-permute-start = (f32[192,416]{1,0:T(8,128)S(1)}, f32[192,416]{1,0:T(8,128)S(1)}, u32[]{:S(2)}, u32[]{:S(2)}) collective-permute-start(f32[192,416]{1,0:T(8,128)S(1)} %pad_select_fusion), channel_id=1, source_target_pairs={{0,64},{64,0},{128,192},{192,128},{256,320},{320,256},{384,448},{4... | collective-permute-start | bytes 958472 | tf_op jit(solution)/shard_map/ppermute | solution.py:63
  26.1 26.8 %all-to-all-start.1 = ((f32[8,384,32]{1,2,0:T(8,128)}), f32[8,384,32]{1,2,0:T(8,128)S(1)}, u32[]{:S(2)}, u32[]{:S(2)}) async-start(f32[8,384,32]{1,2,0:T(8,128)} %broadcast_in_dim.15), calls=%async_computation.1 | async-start | bytes 786432 | tf_op jit(solution)/shard_map/all_to_all | solution.py:44
  29.7 13.2 %collective-permute-start.2 = (f32[192,416]{1,0:T(8,128)S(1)}, f32[192,416]{1,0:T(8,128)S(1)}, u32[]{:S(2)}, u32[]{:S(2)}) collective-permute-start(f32[192,416]{1,0:T(8,128)S(1)} %fusion.8), channel_id=1, source_target_pairs={{0,256},{64,320},{128,384},{192,448},{256,0},{320,64},{384,128},{4... | collective-permute-start | bytes 958472 | tf_op jit(solution)/shard_map/ppermute | solution.py:63
  32.0 20.5 %collective-permute-start.3 = (f32[192,416]{1,0:T(8,128)S(1)}, f32[192,416]{1,0:T(8,128)S(1)}, u32[]{:S(2)}, u32[]{:S(2)}) collective-permute-start(f32[192,416]{1,0:T(8,128)S(1)} %fusion.8), channel_id=1, source_target_pairs={{0,384},{64,448},{128,256},{192,320},{256,128},{320,192},{384,0},{... | collective-permute-start | bytes 958472 | tf_op jit(solution)/shard_map/ppermute | solution.py:63
  36.2 16.3 %collective-permute-start.1 = (f32[192,416]{1,0:T(8,128)S(1)}, f32[192,416]{1,0:T(8,128)S(1)}, u32[]{:S(2)}, u32[]{:S(2)}) collective-permute-start(f32[192,416]{1,0:T(8,128)S(1)} %fusion.8), channel_id=1, source_target_pairs={{0,128},{64,192},{128,0},{192,64},{256,384},{320,448},{384,256},{4... | collective-permute-start | bytes 958472 | tf_op jit(solution)/shard_map/ppermute | solution.py:63
  125.1 7.0 %copy-start.3 = (f32[192,416]{1,0:T(8,128)S(1)}, f32[192,416]{1,0:T(8,128)}, u32[]{:S(2)}) copy-start(f32[192,416]{1,0:T(8,128)} %param.12) | copy-start | bytes 958468
  125.1 7.0 %copy-start.4 = (f32[192,416]{1,0:T(8,128)S(1)}, f32[192,416]{1,0:T(8,128)}, u32[]{:S(2)}) copy-start(f32[192,416]{1,0:T(8,128)} %param.13) | copy-start | bytes 958468
  125.1 6.9 %collective-permute-start.4 = (f32[832,32]{0,1:T(8,128)S(1)}, f32[832,32]{0,1:T(8,128)S(1)}, u32[]{:S(2)}, u32[]{:S(2)}) collective-permute-start(f32[832,32]{0,1:T(8,128)S(1)} %pad_maximum_fusion), channel_id=1, source_target_pairs={{0,64},{64,0},{128,192},{192,128},{256,320},{320,256},{384,448},{4... | collective-permute-start | bytes 319496 | tf_op jit(solution)/shard_map/ppermute | solution.py:138
  132.1 1.7 %copy-start.7 = (f32[416,32]{0,1:T(8,128)}, f32[416,32]{0,1:T(8,128)S(1)}, u32[]{:S(2)}) copy-start(f32[416,32]{0,1:T(8,128)S(1)} %slice.73) | copy-start | bytes 159748
  132.1 1.7 %copy-start.8 = (f32[192,32]{0,1:T(8,128)}, f32[192,32]{0,1:T(8,128)S(1)}, u32[]{:S(2)}) copy-start(f32[192,32]{0,1:T(8,128)S(1)} %slice.75) | copy-start | bytes 73732
  132.1 1.7 %copy-start.5 = (f32[384,192]{0,1:T(8,128)S(1)}, f32[384,192]{0,1:T(8,128)}, u32[]{:S(2)}) copy-start(f32[384,192]{0,1:T(8,128)} %param.17) | copy-start | bytes 884740
  132.1 1.6 %copy-start.6 = (f32[384,192]{0,1:T(8,128)S(1)}, f32[384,192]{0,1:T(8,128)}, u32[]{:S(2)}) copy-start(f32[384,192]{0,1:T(8,128)} %param.18) | copy-start | bytes 884740

commit v7 on v5

--- a/solution.py
+++ b/solution.py
@@ -1,6 +1,7 @@
 import jax
 import jax.numpy as jnp
 from jax import lax
+from jax.experimental import pallas as pl
 from jax.sharding import PartitionSpec as P
 
 
@@ -17,26 +18,28 @@
     return jnp.dot(left, right, precision=lax.Precision.HIGHEST, preferred_element_type=jnp.float32)
 
 
-def batched_dot(left, right):
-    return jnp.einsum(
-        "bij,bjk->bik",
-        left,
-        right,
-        precision=lax.Precision.HIGHEST,
-        preferred_element_type=jnp.float32,
-    )
+def inverse_root_kernel(gram_ref, out_ref):
+    gram = gram_ref[...]
+    size = gram.shape[0]
+    identity = (
+        lax.broadcasted_iota(jnp.int32, (size, size), 0) == lax.broadcasted_iota(jnp.int32, (size, size), 1)
+    ).astype(jnp.float32)
+    squares = jnp.sum(jnp.sum(gram * gram, axis=1, keepdims=True), axis=0, keepdims=True)
+    norm_scale = jnp.sqrt(squares + EPSILON)
+    current = gram / norm_scale
+    inverse = identity
+    for _ in range(NS_STEPS):
+        middle = 0.5 * (3.0 * identity - precise_dot(inverse, current))
+        current = precise_dot(current, middle)
+        inverse = precise_dot(middle, inverse)
+    out_ref[...] = inverse / jnp.sqrt(norm_scale)
 
 
 def inverse_root(gram_sum):
-    identity = jnp.eye(gram_sum.shape[-1], dtype=jnp.float32)[None]
-    norm_scale = jnp.sqrt(jnp.sum(gram_sum * gram_sum, axis=(1, 2), keepdims=True) + EPSILON)
-    current = gram_sum / norm_scale
-    inverse = jnp.broadcast_to(identity, gram_sum.shape)
-    for _ in range(NS_STEPS):
-        middle = 0.5 * (3.0 * identity - batched_dot(inverse, current))
-        current = batched_dot(current, middle)
-        inverse = batched_dot(middle, inverse)
-    return inverse / jnp.sqrt(norm_scale)
+    return pl.pallas_call(
+        inverse_root_kernel,
+        out_shape=jax.ShapeDtypeStruct(gram_sum.shape, jnp.float32),
+    )(gram_sum)
 
 
 def gather_sum(x, axis):
@@ -117,7 +120,7 @@
         mine = pick(pad_rows(side_in, col_pad), pad_rows(side_out, col_pad))
         column = gather_sum(mine, "shard")
         gram = pick(column[cols[0] : cols[0] + rank], column[cols[1] : cols[1] + rank])
-        inverse = inverse_root(gram[None])[0]
+        inverse = inverse_root(gram)
         return precise_dot(projected, inverse), precise_dot(column, inverse) / replicas
 
     partial = jnp.concatenate([precise_dot(m, q) for m, q in zip(merged, (inproj_query, outproj_query))], axis=0)

time: 132 us -> 135 us (1.023)
  Pallas kernels: 0 us -> 5.41 us
  matrix products: 10.9 us -> 9.08 us
  between operations: 2.73 us -> 1.11 us
    pallas_call x0 -> x2, Pallas kernels: none -> 5.41 us  [inverse_root(): pl.pallas_call(inverse_root_kernel, out_shape=jax.ShapeDtypeStruct(gram_s...]
    dot_general x22 -> x0, matrix products: 3.31 us -> none  [batched_dot(): jnp.einsum('bij,bjk->bik', left, right, precision=lax.Precision.HIGHEST,...]
    dot_general x13, matrix products: 6.23 us -> 7.72 us  [precise_dot(): jnp.dot(left, right, precision=lax.Precision.HIGHEST, preferred_element_t...]
    reduce_sum x2 -> x0, other arithmetic: 1.36 us -> none  [inverse_root(): jnp.sum(gram_sum * gram_sum, axis=(1, 2), keepdims=True) + EPSILON]
where the time goes in v7:
time: 135 us; the launch traced here: 134 us
  blocking collectives  54.8 us (41%)
  starting transfers between devices  28.8 us (21%)
  waiting for transfers between devices  28.2 us (21%)
  matrix products  9.08 us (7%)
  Pallas kernels  5.41 us (4%)
  local copies, waits for them, and re-layouts  3.33 us (2%)
  other arithmetic  3.15 us (2%)
    all_to_all x3, blocking collectives, gather_sum(): lax.all_to_all(jnp.broadcast_to(x[None], (n,) + x.shape), axis, 0, 0, til...  54.8 us
    ppermute x3, waiting for transfers between devices, replica_total(): moved = lax.ppermute(sent, 'replica', pairs)  18.8 us
    all_to_all x2, starting transfers between devices, gather_sum(): lax.all_to_all(jnp.broadcast_to(x[None], (n,) + x.shape), axis, 0, 0, til...  13.7 us
    all_to_all x2, waiting for transfers between devices, gather_sum(): lax.all_to_all(jnp.broadcast_to(x[None], (n,) + x.shape), axis, 0, 0, til...  8.37 us
    ppermute x1, starting transfers between devices, per_device(): other = lax.ppermute(held, 'replica', [(i, i ^ 1) for i in range(n)])  8.08 us
    dot_general x13, matrix products, precise_dot(): jnp.dot(left, right, precision=lax.Precision.HIGHEST, preferred_element_t...  7.72 us
    ppermute x3, starting transfers between devices, replica_total(): moved = lax.ppermute(sent, 'replica', pairs)  7.01 us
    pallas_call x2, Pallas kernels, inverse_root(): pl.pallas_call(inverse_root_kernel, out_shape=jax.ShapeDtypeStruct(gram_s...  5.41 us
  transfers between devices with their start and end apart: 6, of which 4 were waited for; matrix products, arithmetic and copies ran while one was open for 1% of the time, Pallas kernels for 0%

profile of v7, /device:TPU:1, one launch (start us, length us, event | category | flops | bytes accessed | tf_op | source)
XLA Modules:
  0.0 133.9 jit_solution(15278257246350609063)
XLA Ops:
  0.7 1.1 convert_add_fusion.1
  1.8 0.3 fusion.4
  2.1 0.6 copy-done.2
  2.7 0.5 fusion.1
  3.2 0.1 pad_maximum_fusion.1
  3.3 0.9 broadcast_in_dim.14
  4.2 10.3 %all-to-all-start = ((f32[8,576,32]{1,2,0:T(8,128)}), f32[8,576,32]{1,2,0:T(8,128)S(1)}, u32[]{:S(2)}, u32[]{:S(2)}) async-start(f32[8,576,32]{1,2,0:T(8,128)} %broadcast_in_dim.14), calls=%async_computation | async-start | bytes 1310720 | tf_op jit(solution)/shard_map/all_to_all | solution.py:47
  14.4 0.2 copy.31
  14.6 0.1 add.47
  14.8 2.0 %collective-permute-start = (f32[192,416]{1,0:T(8,128)S(1)}, f32[192,416]{1,0:T(8,128)S(1)}, u32[]{:S(2)}, u32[]{:S(2)}) collective-permute-start(f32[192,416]{1,0:T(8,128)S(1)} %pad_select_fusion), channel_id=1, source_target_pairs={{0,64},{64,0},{128,192},{192,128},{256,320},{320,256},{384,448},{4... | collective-permute-start | bytes 958472 | tf_op jit(solution)/shard_map/ppermute | solution.py:67
  16.9 8.4 %all-to-all-done = f32[8,576,32]{1,2,0:T(8,128)S(1)} async-done(((f32[8,576,32]{1,2,0:T(8,128)}), f32[8,576,32]{1,2,0:T(8,128)S(1)}, u32[]{:S(2)}, u32[]{:S(2)}) %all-to-all-start) | async-done | bytes 589856 | tf_op jit(solution)/shard_map/all_to_all | solution.py:47
  25.3 0.1 slice_select_fusion
  25.4 0.8 broadcast_in_dim.15
  26.1 3.5 %all-to-all-start.1 = ((f32[8,384,32]{1,2,0:T(8,128)}), f32[8,384,32]{1,2,0:T(8,128)S(1)}, u32[]{:S(2)}, u32[]{:S(2)}) async-start(f32[8,384,32]{1,2,0:T(8,128)} %broadcast_in_dim.15), calls=%async_computation.1 | async-start | bytes 786432 | tf_op jit(solution)/shard_map/all_to_all | solution.py:47
  29.6 0.1 fusion
  29.7 2.2 %collective-permute-start.1 = (f32[192,416]{1,0:T(8,128)S(1)}, f32[192,416]{1,0:T(8,128)S(1)}, u32[]{:S(2)}, u32[]{:S(2)}) collective-permute-start(f32[192,416]{1,0:T(8,128)S(1)} %fusion), channel_id=1, source_target_pairs={{0,128},{64,192},{128,0},{192,64},{256,384},{320,448},{384,256},{4... | collective-permute-start | bytes 958472 | tf_op jit(solution)/shard_map/ppermute | solution.py:67
  31.9 9.4 %collective-permute-done.1 = f32[192,416]{1,0:T(8,128)S(1)} collective-permute-done((f32[192,416]{1,0:T(8,128)S(1)}, f32[192,416]{1,0:T(8,128)S(1)}, u32[]{:S(2)}, u32[]{:S(2)}) %collective-permute-start.1) | collective-permute-done | bytes 319520 | tf_op jit(solution)/shard_map/ppermute | solution.py:67
  41.4 2.8 %collective-permute-start.2 = (f32[192,416]{1,0:T(8,128)S(1)}, f32[192,416]{1,0:T(8,128)S(1)}, u32[]{:S(2)}, u32[]{:S(2)}) collective-permute-start(f32[192,416]{1,0:T(8,128)S(1)} %add.49), channel_id=1, source_target_pairs={{0,256},{64,320},{128,384},{192,448},{256,0},{320,64},{384,128},{4... | collective-permute-start | bytes 958472 | tf_op jit(solution)/shard_map/ppermute | solution.py:67
  44.2 9.5 %collective-permute-done.2 = f32[192,416]{1,0:T(8,128)S(1)} collective-permute-done((f32[192,416]{1,0:T(8,128)S(1)}, f32[192,416]{1,0:T(8,128)S(1)}, u32[]{:S(2)}, u32[]{:S(2)}) %collective-permute-start.2) | collective-permute-done | bytes 319520 | tf_op jit(solution)/shard_map/ppermute | solution.py:67
  53.7 0.1 reshape.33
  53.9 0.2 fusion.27
  54.1 0.2 fusion.23
  54.3 0.3 fusion.25
  54.6 0.3 fusion.28
  55.0 0.1 fusion.10
  55.1 21.6 %all_to_all.25 = f32[8,448,32]{1,2,0:T(8,128)S(1)} all-to-all(f32[8,448,32]{1,2,0:T(8,128)S(1)} %broadcast_in_dim.16), channel_id=1, replica_groups=mesh['replica'=8,'shard'=8,'tensor'=8] {'shard'}, dimensions={0} | all-to-all | bytes 917504 | tf_op jit(solution)/shard_map/all_to_all | solution.py:47
  76.7 0.1 fusion.33
  77.0 0.6 broadcast_select_fusion.3.gram_ref
  77.6 2.7 %shard_map.161 = f32[32,32]{1,0:T(8,128)} custom-call(f32[32,32]{1,0:T(8,128)} %broadcast_select_fusion.3.gram_ref), custom_call_target="tpu_custom_call" | custom-call | tf_op jit(solution)/shard_map/pallas_call | solution.py:39
  80.3 1.0 convolution_multiply_fusion.1
  81.3 0.5 fusion.8
  81.7 0.5 pad_select_fusion.2
  82.3 16.3 %all_to_all.26 = f32[8,384,32]{1,2,0:T(8,128)S(1)} all-to-all(f32[8,384,32]{1,2,0:T(8,128)S(1)} %broadcast_in_dim.17), channel_id=1, replica_groups=mesh['replica'=8,'shard'=8,'tensor'=8] {'tensor'}, dimensions={0} | all-to-all | bytes 786432 | tf_op jit(solution)/shard_map/all_to_all | solution.py:47
  98.6 0.2 fusion.30
  98.8 0.3 fusion.31
  99.1 0.2 fusion.19
  99.3 0.3 fusion.21
  99.7 0.1 fusion.7
  99.8 16.9 %all_to_all.27 = f32[8,448,32]{1,2,0:T(8,128)S(1)} all-to-all(f32[8,448,32]{1,2,0:T(8,128)S(1)} %broadcast_in_dim.18), channel_id=1, replica_groups=mesh['replica'=8,'shard'=8,'tensor'=8] {'shard'}, dimensions={0} | all-to-all | bytes 917504 | tf_op jit(solution)/shard_map/all_to_all | solution.py:47
  116.8 0.1 fusion.32
  117.0 0.6 broadcast_select_fusion.2.gram_ref
  117.6 2.7 %shard_map.162 = f32[32,32]{1,0:T(8,128)} custom-call(f32[32,32]{1,0:T(8,128)} %broadcast_select_fusion.2.gram_ref), custom_call_target="tpu_custom_call" | custom-call | tf_op jit(solution)/shard_map/pallas_call | solution.py:39
  120.3 1.0 convolution_multiply_fusion
  121.4 0.2 fusion.29
  121.7 8.1 %collective-permute-start.3 = (f32[832,32]{0,1:T(8,128)S(1)}, f32[832,32]{0,1:T(8,128)S(1)}, u32[]{:S(2)}, u32[]{:S(2)}) collective-permute-start(f32[832,32]{0,1:T(8,128)S(1)} %pad_maximum_fusion), channel_id=1, source_target_pairs={{0,64},{64,0},{128,192},{192,128},{256,320},{320,256},{384,448},{4... | collective-permute-start | bytes 319496 | tf_op jit(solution)/shard_map/ppermute | solution.py:139
  129.8 0.9 collective-permute-done.3
  130.8 1.6 %multiply_subtract_fusion = (f32[192,416]{1,0:T(8,128)}, f32[192,416]{1,0:T(8,128)}, f32[1,192,416]{2,1,0:T(8,128)}) fusion(f32[192,416]{1,0:T(8,128)S(1)} %copy-done.3, f32[192,416]{1,0:T(8,128)S(1)} %copy-done.4, f32[1,192,416]{2,1,0:T(8,128)S(1)} %copy-done.1, bf16[1,192,416]{2,1,0:T(8,128)(2,1)S(1)} %copy-done.2, f32[416,32]{0,1:T(8,128)S(1)} %slice.73, ...), kind=kOutput, calls=%fused_computation.9 | convolution fusion | flops 31229952 | bytes 2433024 | tf_op jit(solution)/shard_map/dot_general | solution.py:18
  132.5 1.4 %multiply_subtract_fusion.1 = (f32[384,192]{0,1:T(8,128)}, f32[384,192]{0,1:T(8,128)}, f32[1,384,192]{1,2,0:T(8,128)}) fusion(f32[384,192]{0,1:T(8,128)S(1)} %copy-done.5, f32[384,192]{0,1:T(8,128)S(1)} %copy-done.6, f32[1,384,192]{1,2,0:T(8,128)S(1)} %convert_add_fusion.1, f32[192,32]{0,1:T(8,128)S(1)} %slice.75, f32[832,32]{0,1:T(8,128)S(1)} %get-tuple-element.14), kind=kOutput, calls=%fused_computation.16 | convolution fusion | flops 28680192 | bytes 1851392 | tf_op jit(solution)/shard_map/dot_general | solution.py:18
  (47 shorter events, 0.9 us)
Async XLA Ops:
  0.6 1.5 %copy-start = (f32[416,32]{0,1:T(8,128)S(1)}, f32[416,32]{0,1:T(8,128)}, u32[]{:S(2)}) copy-start(f32[416,32]{0,1:T(8,128)} %param.14) | copy-start | bytes 159748
  0.6 1.1 copy-start.10
  0.7 1.5 %copy-start.1 = (f32[1,192,416]{2,1,0:T(8,128)S(1)}, f32[1,192,416]{2,1,0:T(8,128)}, u32[]{:S(2)}) copy-start(f32[1,192,416]{2,1,0:T(8,128)} %param.11) | copy-start | bytes 958468
  1.8 1.0 copy-start.2
  4.2 21.1 %all-to-all-start = ((f32[8,576,32]{1,2,0:T(8,128)}), f32[8,576,32]{1,2,0:T(8,128)S(1)}, u32[]{:S(2)}, u32[]{:S(2)}) async-start(f32[8,576,32]{1,2,0:T(8,128)} %broadcast_in_dim.14), calls=%async_computation | async-start | bytes 1310720 | tf_op jit(solution)/shard_map/all_to_all | solution.py:47
  14.8 10.4 %copy-start.11 = (pred[384]{0:T(512)(128)(4,1)S(1)}, pred[384]{0:T(512)(128)(4,1)}, u32[]{:S(2)}) copy-start(pred[384]{0:T(512)(128)(4,1)} %constant.35.clone.1) | copy-start | bytes 1156
  14.8 14.8 %collective-permute-start = (f32[192,416]{1,0:T(8,128)S(1)}, f32[192,416]{1,0:T(8,128)S(1)}, u32[]{:S(2)}, u32[]{:S(2)}) collective-permute-start(f32[192,416]{1,0:T(8,128)S(1)} %pad_select_fusion), channel_id=1, source_target_pairs={{0,64},{64,0},{128,192},{192,128},{256,320},{320,256},{384,448},{4... | collective-permute-start | bytes 958472 | tf_op jit(solution)/shard_map/ppermute | solution.py:67
  26.1 27.7 %all-to-all-start.1 = ((f32[8,384,32]{1,2,0:T(8,128)}), f32[8,384,32]{1,2,0:T(8,128)S(1)}, u32[]{:S(2)}, u32[]{:S(2)}) async-start(f32[8,384,32]{1,2,0:T(8,128)} %broadcast_in_dim.15), calls=%async_computation.1 | async-start | bytes 786432 | tf_op jit(solution)/shard_map/all_to_all | solution.py:47
  29.7 11.6 %collective-permute-start.1 = (f32[192,416]{1,0:T(8,128)S(1)}, f32[192,416]{1,0:T(8,128)S(1)}, u32[]{:S(2)}, u32[]{:S(2)}) collective-permute-start(f32[192,416]{1,0:T(8,128)S(1)} %fusion), channel_id=1, source_target_pairs={{0,128},{64,192},{128,0},{192,64},{256,384},{320,448},{384,256},{4... | collective-permute-start | bytes 958472 | tf_op jit(solution)/shard_map/ppermute | solution.py:67
  41.4 12.3 %collective-permute-start.2 = (f32[192,416]{1,0:T(8,128)S(1)}, f32[192,416]{1,0:T(8,128)S(1)}, u32[]{:S(2)}, u32[]{:S(2)}) collective-permute-start(f32[192,416]{1,0:T(8,128)S(1)} %add.49), channel_id=1, source_target_pairs={{0,256},{64,320},{128,384},{192,448},{256,0},{320,64},{384,128},{4... | collective-permute-start | bytes 958472 | tf_op jit(solution)/shard_map/ppermute | solution.py:67
  120.3 1.0 copy-start.8
  121.6 9.1 %copy-start.3 = (f32[192,416]{1,0:T(8,128)S(1)}, f32[192,416]{1,0:T(8,128)}, u32[]{:S(2)}) copy-start(f32[192,416]{1,0:T(8,128)} %param.12) | copy-start | bytes 958468
  121.6 9.1 %copy-start.4 = (f32[192,416]{1,0:T(8,128)S(1)}, f32[192,416]{1,0:T(8,128)}, u32[]{:S(2)}) copy-start(f32[192,416]{1,0:T(8,128)} %param.13) | copy-start | bytes 958468
  121.7 9.0 %collective-permute-start.3 = (f32[832,32]{0,1:T(8,128)S(1)}, f32[832,32]{0,1:T(8,128)S(1)}, u32[]{:S(2)}, u32[]{:S(2)}) collective-permute-start(f32[832,32]{0,1:T(8,128)S(1)} %pad_maximum_fusion), channel_id=1, source_target_pairs={{0,64},{64,0},{128,192},{192,128},{256,320},{320,256},{384,448},{4... | collective-permute-start | bytes 319496 | tf_op jit(solution)/shard_map/ppermute | solution.py:139
  130.7 1.7 %copy-start.7 = (f32[416,32]{0,1:T(8,128)}, f32[416,32]{0,1:T(8,128)S(1)}, u32[]{:S(2)}) copy-start(f32[416,32]{0,1:T(8,128)S(1)} %slice.73) | copy-start | bytes 159748
  130.8 1.7 %copy-start.9 = (f32[192,32]{0,1:T(8,128)}, f32[192,32]{0,1:T(8,128)S(1)}, u32[]{:S(2)}) copy-start(f32[192,32]{0,1:T(8,128)S(1)} %slice.75) | copy-start | bytes 73732
  130.8 1.7 %copy-start.5 = (f32[384,192]{0,1:T(8,128)S(1)}, f32[384,192]{0,1:T(8,128)}, u32[]{:S(2)}) copy-start(f32[384,192]{0,1:T(8,128)} %param.17) | copy-start | bytes 884740
  130.8 1.7 %copy-start.6 = (f32[384,192]{0,1:T(8,128)S(1)}, f32[384,192]{0,1:T(8,128)}, u32[]{:S(2)}) copy-start(f32[384,192]{0,1:T(8,128)} %param.18) | copy-start | bytes 884740

commit v8 on v5

--- a/solution.py
+++ b/solution.py
@@ -120,9 +120,12 @@
         inverse = inverse_root(gram[None])[0]
         return precise_dot(projected, inverse), precise_dot(column, inverse) / replicas
 
-    partial = jnp.concatenate([precise_dot(m, q) for m, q in zip(merged, (inproj_query, outproj_query))], axis=0)
-    summed = gather_sum(partial, "replica")
-    mine = pick(pad_rows(summed[: rows[0]], row_pad), pad_rows(summed[rows[0] :], row_pad))
+    part_in = pad_rows(precise_dot(merged[0], inproj_query), row_pad)
+    part_out = pad_rows(precise_dot(merged[1], outproj_query), row_pad)
+    n = lax.axis_size("replica")
+    to_first = (lax.broadcasted_iota(jnp.int32, (n, 1, 1), 0) % 2) == 0
+    outgoing = jnp.where(to_first, part_in[None], part_out[None])
+    mine = jnp.sum(lax.all_to_all(outgoing, "replica", 0, 0, tiled=False), axis=0)
     projected = gather_sum(mine, "tensor") / replicas
     ortho, query = column_step(projected)
     for _ in range(1, ROUNDS):
@@ -132,7 +135,6 @@
         projected = gather_sum(mine, "tensor") / replicas
         ortho, query = column_step(projected)
     held = jnp.concatenate([ortho, query], axis=0)
-    n = lax.axis_size("replica")
     other = lax.ppermute(held, "replica", [(i, i ^ 1) for i in range(n)])
     own_in = pick(held, other)
     own_out = pick(other, held)

time: 132 us -> 130 us (0.985)
  waiting for transfers between devices: 28.2 us -> 23.6 us
  local copies, waits for them, and re-layouts: 2.87 us -> 4.42 us
    all_to_all x2 -> x1, starting transfers between devices: 13.7 us -> 3.45 us  [gather_sum(): lax.all_to_all(jnp.broadcast_to(x[None], (n,) + x.shape), axis, 0, 0, til...]
    all_to_all x0 -> x1, starting transfers between devices: none -> 10.2 us  [per_device(): lax.all_to_all(outgoing, 'replica', 0, 0, tiled=False)]
    all_to_all x2 -> x1, waiting for transfers between devices: 8.37 us -> 0.01 us  [gather_sum(): lax.all_to_all(jnp.broadcast_to(x[None], (n,) + x.shape), axis, 0, 0, til...]
    all_to_all x0 -> x1, waiting for transfers between devices: none -> 4.41 us  [per_device(): lax.all_to_all(outgoing, 'replica', 0, 0, tiled=False)]
    unnamed x22 -> x24, local copies, waits for them, and re-layouts: 0.64 us -> 3.07 us
where the time goes in v8:
time: 130 us; the launch traced here: 129 us
  blocking collectives  54.8 us (42%)
  starting transfers between devices  28.7 us (22%)
  waiting for transfers between devices  23.6 us (18%)
  matrix products  12 us (9%)
  local copies, waits for them, and re-layouts  4.42 us (3%)
  other arithmetic  2.87 us (2%)
  between operations  2.63 us (2%)
    all_to_all x3, blocking collectives, gather_sum(): lax.all_to_all(jnp.broadcast_to(x[None], (n,) + x.shape), axis, 0, 0, til...  54.8 us
    ppermute x3, waiting for transfers between devices, replica_total(): moved = lax.ppermute(sent, 'replica', pairs)  18.2 us
    all_to_all x1, starting transfers between devices, per_device(): lax.all_to_all(outgoing, 'replica', 0, 0, tiled=False)  10.2 us
    ppermute x1, starting transfers between devices, per_device(): other = lax.ppermute(held, 'replica', [(i, i ^ 1) for i in range(n)])  7.95 us
    dot_general x13, matrix products, precise_dot(): jnp.dot(left, right, precision=lax.Precision.HIGHEST, preferred_element_t...  7.32 us
    ppermute x3, starting transfers between devices, replica_total(): moved = lax.ppermute(sent, 'replica', pairs)  7.14 us
    all_to_all x1, waiting for transfers between devices, per_device(): lax.all_to_all(outgoing, 'replica', 0, 0, tiled=False)  4.41 us
    all_to_all x1, starting transfers between devices, gather_sum(): lax.all_to_all(jnp.broadcast_to(x[None], (n,) + x.shape), axis, 0, 0, til...  3.45 us
  transfers between devices with their start and end apart: 6, of which 4 were waited for; matrix products, arithmetic and copies ran while one was open for 1% of the time, Pallas kernels for 0%

profile of v8, /device:TPU:1, one launch (start us, length us, event | category | flops | bytes accessed | tf_op | source)
XLA Modules:
  0.0 129.1 jit_solution(8298286516021456514)
XLA Ops:
  0.7 0.8 copy-done
  1.5 1.6 %fusion.9 = f32[192,32]{0,1:T(8,128)S(1)} fusion(f32[416,32]{0,1:T(8,128)S(1)} %copy-done, f32[1,192,416]{2,1,0:T(8,128)} %param.11, bf16[1,192,416]{2,1,0:T(8,128)(2,1)} %param.10), kind=kOutput, calls=%fused_computation.24 | convolution fusion | flops 30830592 | bytes 557056 | tf_op jit(solution)/shard_map/dot_general | solution.py:17
  3.1 0.7 copy-done.11
  3.8 0.3 fusion.12
  4.2 0.8 broadcast_select_fusion
  5.0 10.2 %all-to-all-start = ((f32[8,384,32]{1,2,0:T(8,128)}), f32[8,384,32]{1,2,0:T(8,128)S(1)}, u32[]{:S(2)}, u32[]{:S(2)}) async-start(f32[8,384,32]{1,2,0:T(8,128)} %broadcast_select_fusion), calls=%async_computation | async-start | bytes 786432 | tf_op jit(solution)/shard_map/all_to_all | solution.py:128
  15.2 0.2 copy.31
  15.6 0.8 copy-done.1
  16.5 2.0 %collective-permute-start = (f32[192,416]{1,0:T(8,128)S(1)}, f32[192,416]{1,0:T(8,128)S(1)}, u32[]{:S(2)}, u32[]{:S(2)}) collective-permute-start(f32[192,416]{1,0:T(8,128)S(1)} %pad_select_fusion), channel_id=1, source_target_pairs={{0,64},{64,0},{128,192},{192,128},{256,320},{320,256},{384,448},{4... | collective-permute-start | bytes 958472 | tf_op jit(solution)/shard_map/ppermute | solution.py:64
  18.5 4.4 %all-to-all-done = f32[8,384,32]{1,2,0:T(8,128)S(1)} async-done(((f32[8,384,32]{1,2,0:T(8,128)}), f32[8,384,32]{1,2,0:T(8,128)S(1)}, u32[]{:S(2)}, u32[]{:S(2)}) %all-to-all-start) | async-done | bytes 393248 | tf_op jit(solution)/shard_map/all_to_all | solution.py:128
  23.0 0.8 broadcast_in_dim.39
  23.8 3.5 %all-to-all-start.1 = ((f32[8,384,32]{1,2,0:T(8,128)}), f32[8,384,32]{1,2,0:T(8,128)S(1)}, u32[]{:S(2)}, u32[]{:S(2)}) async-start(f32[8,384,32]{1,2,0:T(8,128)} %broadcast_in_dim.39), calls=%async_computation.1 | async-start | bytes 786432 | tf_op jit(solution)/shard_map/all_to_all | solution.py:44
  27.3 2.2 %collective-permute-start.1 = (f32[192,416]{1,0:T(8,128)S(1)}, f32[192,416]{1,0:T(8,128)S(1)}, u32[]{:S(2)}, u32[]{:S(2)}) collective-permute-start(f32[192,416]{1,0:T(8,128)S(1)} %fusion.8), channel_id=1, source_target_pairs={{0,128},{64,192},{128,0},{192,64},{256,384},{320,448},{384,256},{4... | collective-permute-start | bytes 958472 | tf_op jit(solution)/shard_map/ppermute | solution.py:64
  29.5 9.1 %collective-permute-done.1 = f32[192,416]{1,0:T(8,128)S(1)} collective-permute-done((f32[192,416]{1,0:T(8,128)S(1)}, f32[192,416]{1,0:T(8,128)S(1)}, u32[]{:S(2)}, u32[]{:S(2)}) %collective-permute-start.1) | collective-permute-done | bytes 319520 | tf_op jit(solution)/shard_map/ppermute | solution.py:64
  38.7 2.9 %collective-permute-start.2 = (f32[192,416]{1,0:T(8,128)S(1)}, f32[192,416]{1,0:T(8,128)S(1)}, u32[]{:S(2)}, u32[]{:S(2)}) collective-permute-start(f32[192,416]{1,0:T(8,128)S(1)} %add.70), channel_id=1, source_target_pairs={{0,256},{64,320},{128,384},{192,448},{256,0},{320,64},{384,128},{4... | collective-permute-start | bytes 958472 | tf_op jit(solution)/shard_map/ppermute | solution.py:64
  41.7 9.1 %collective-permute-done.2 = f32[192,416]{1,0:T(8,128)S(1)} collective-permute-done((f32[192,416]{1,0:T(8,128)S(1)}, f32[192,416]{1,0:T(8,128)S(1)}, u32[]{:S(2)}, u32[]{:S(2)}) %collective-permute-start.2) | collective-permute-done | bytes 319520 | tf_op jit(solution)/shard_map/ppermute | solution.py:64
  51.0 0.2 fusion.40
  51.2 0.2 fusion.31
  51.4 0.3 fusion.33
  51.7 0.3 fusion.41
  52.2 21.3 %all_to_all.25 = f32[8,448,32]{1,2,0:T(8,128)S(1)} all-to-all(f32[8,448,32]{1,2,0:T(8,128)S(1)} %broadcast_in_dim.40), channel_id=1, replica_groups=mesh['replica'=8,'shard'=8,'tensor'=8] {'shard'}, dimensions={0} | all-to-all | bytes 917504 | tf_op jit(solution)/shard_map/all_to_all | solution.py:44
  73.6 0.7 multiply_reduce_fusion.1
  75.1 0.2 fusion.37
  75.5 0.2 fusion.6
  75.8 0.1 fusion.49
  75.9 0.2 fusion.5
  76.4 0.2 fusion.4
  76.7 0.3 convolution_multiply_fusion.1
  77.0 0.5 fusion.16
  77.4 0.5 pad_select_fusion.2
  78.0 16.6 %all_to_all.26 = f32[8,384,32]{1,2,0:T(8,128)S(1)} all-to-all(f32[8,384,32]{1,2,0:T(8,128)S(1)} %broadcast_in_dim.41), channel_id=1, replica_groups=mesh['replica'=8,'shard'=8,'tensor'=8] {'tensor'}, dimensions={0} | all-to-all | bytes 786432 | tf_op jit(solution)/shard_map/all_to_all | solution.py:44
  94.6 0.3 fusion.44
  95.0 0.2 fusion.43
  95.2 0.3 fusion.29
  95.6 0.2 fusion.27
  95.9 16.9 %all_to_all.27 = f32[8,448,32]{1,2,0:T(8,128)S(1)} all-to-all(f32[8,448,32]{1,2,0:T(8,128)S(1)} %broadcast_in_dim.42), channel_id=1, replica_groups=mesh['replica'=8,'shard'=8,'tensor'=8] {'shard'}, dimensions={0} | all-to-all | bytes 917504 | tf_op jit(solution)/shard_map/all_to_all | solution.py:44
  112.8 0.7 multiply_reduce_fusion
  114.3 0.2 fusion.38
  114.7 0.2 fusion.2
  115.2 0.2 fusion.1
  115.6 0.2 fusion
  115.9 0.3 convolution_multiply_fusion
  116.2 0.2 fusion.42
  116.5 7.9 %collective-permute-start.3 = (f32[832,32]{0,1:T(8,128)S(1)}, f32[832,32]{0,1:T(8,128)S(1)}, u32[]{:S(2)}, u32[]{:S(2)}) collective-permute-start(f32[832,32]{0,1:T(8,128)S(1)} %pad_maximum_fusion), channel_id=1, source_target_pairs={{0,64},{64,0},{128,192},{192,128},{256,320},{320,256},{384,448},{4... | collective-permute-start | bytes 319496 | tf_op jit(solution)/shard_map/ppermute | solution.py:138
  124.5 0.9 collective-permute-done.3
  125.5 0.6 copy-done.10
  126.1 1.4 %multiply_subtract_fusion.1 = (f32[384,192]{0,1:T(8,128)}, f32[384,192]{0,1:T(8,128)}, f32[1,384,192]{1,2,0:T(8,128)}) fusion(f32[384,192]{0,1:T(8,128)S(1)} %copy-done.5, f32[384,192]{0,1:T(8,128)S(1)} %copy-done.6, f32[1,384,192]{1,2,0:T(8,128)S(1)} %convert_add_fusion.1, f32[192,32]{0,1:T(8,128)S(1)} %slice.64, f32[832,32]{0,1:T(8,128)S(1)} %get-tuple-element.18), kind=kOutput, calls=%fused_computation.34 | convolution fusion | flops 28680192 | bytes 1851392 | tf_op jit(solution)/shard_map/dot_general | solution.py:17
  127.5 1.6 %multiply_subtract_fusion = (f32[192,416]{1,0:T(8,128)}, f32[192,416]{1,0:T(8,128)}, f32[1,192,416]{2,1,0:T(8,128)}) fusion(f32[192,416]{1,0:T(8,128)S(1)} %copy-done.3, f32[192,416]{1,0:T(8,128)S(1)} %copy-done.4, f32[1,192,416]{2,1,0:T(8,128)S(1)} %copy-done.1, bf16[1,192,416]{2,1,0:T(8,128)(2,1)S(1)} %copy-done.2, f32[416,32]{0,1:T(8,128)S(1)} %slice.62, ...), kind=kOutput, calls=%fused_computation.27 | convolution fusion | flops 31229952 | bytes 2433024 | tf_op jit(solution)/shard_map/dot_general | solution.py:17
  (61 shorter events, 3.0 us)
Async XLA Ops:
  0.6 0.8 copy-start
  1.5 1.6 %copy-start.7 = (f32[1,384,192]{1,2,0:T(8,128)S(1)}, f32[1,384,192]{1,2,0:T(8,128)}, u32[]{:S(2)}) copy-start(f32[1,384,192]{1,2,0:T(8,128)} %param.16) | copy-start | bytes 884740
  1.5 1.6 %copy-start.9 = (bf16[1,384,192]{1,2,0:T(8,128)(2,1)S(1)}, bf16[1,384,192]{1,2,0:T(8,128)(2,1)}, u32[]{:S(2)}) copy-start(bf16[1,384,192]{1,2,0:T(8,128)(2,1)} %param.15) | copy-start | bytes 442372
  3.1 0.8 copy-start.11
  5.0 17.9 %all-to-all-start = ((f32[8,384,32]{1,2,0:T(8,128)}), f32[8,384,32]{1,2,0:T(8,128)S(1)}, u32[]{:S(2)}, u32[]{:S(2)}) async-start(f32[8,384,32]{1,2,0:T(8,128)} %broadcast_select_fusion), calls=%async_computation | async-start | bytes 786432 | tf_op jit(solution)/shard_map/all_to_all | solution.py:128
  15.4 1.0 copy-start.1
  15.4 1.0 copy-start.2
  16.5 10.7 %collective-permute-start = (f32[192,416]{1,0:T(8,128)S(1)}, f32[192,416]{1,0:T(8,128)S(1)}, u32[]{:S(2)}, u32[]{:S(2)}) collective-permute-start(f32[192,416]{1,0:T(8,128)S(1)} %pad_select_fusion), channel_id=1, source_target_pairs={{0,64},{64,0},{128,192},{192,128},{256,320},{320,256},{384,448},{4... | collective-permute-start | bytes 958472 | tf_op jit(solution)/shard_map/ppermute | solution.py:64
  23.8 27.2 %all-to-all-start.1 = ((f32[8,384,32]{1,2,0:T(8,128)}), f32[8,384,32]{1,2,0:T(8,128)S(1)}, u32[]{:S(2)}, u32[]{:S(2)}) async-start(f32[8,384,32]{1,2,0:T(8,128)} %broadcast_in_dim.39), calls=%async_computation.1 | async-start | bytes 786432 | tf_op jit(solution)/shard_map/all_to_all | solution.py:44
  27.3 11.3 %collective-permute-start.1 = (f32[192,416]{1,0:T(8,128)S(1)}, f32[192,416]{1,0:T(8,128)S(1)}, u32[]{:S(2)}, u32[]{:S(2)}) collective-permute-start(f32[192,416]{1,0:T(8,128)S(1)} %fusion.8), channel_id=1, source_target_pairs={{0,128},{64,192},{128,0},{192,64},{256,384},{320,448},{384,256},{4... | collective-permute-start | bytes 958472 | tf_op jit(solution)/shard_map/ppermute | solution.py:64
  38.7 12.0 %collective-permute-start.2 = (f32[192,416]{1,0:T(8,128)S(1)}, f32[192,416]{1,0:T(8,128)S(1)}, u32[]{:S(2)}, u32[]{:S(2)}) collective-permute-start(f32[192,416]{1,0:T(8,128)S(1)} %add.70), channel_id=1, source_target_pairs={{0,256},{64,320},{128,384},{192,448},{256,0},{320,64},{384,128},{4... | collective-permute-start | bytes 958472 | tf_op jit(solution)/shard_map/ppermute | solution.py:64
  116.5 9.6 %copy-start.5 = (f32[384,192]{0,1:T(8,128)S(1)}, f32[384,192]{0,1:T(8,128)}, u32[]{:S(2)}) copy-start(f32[384,192]{0,1:T(8,128)} %param.17) | copy-start | bytes 884740
  116.5 9.6 %copy-start.6 = (f32[384,192]{0,1:T(8,128)S(1)}, f32[384,192]{0,1:T(8,128)}, u32[]{:S(2)}) copy-start(f32[384,192]{0,1:T(8,128)} %param.18) | copy-start | bytes 884740
  116.5 8.9 %collective-permute-start.3 = (f32[832,32]{0,1:T(8,128)S(1)}, f32[832,32]{0,1:T(8,128)S(1)}, u32[]{:S(2)}, u32[]{:S(2)}) collective-permute-start(f32[832,32]{0,1:T(8,128)S(1)} %pad_maximum_fusion), channel_id=1, source_target_pairs={{0,64},{64,0},{128,192},{192,128},{256,320},{320,256},{384,448},{4... | collective-permute-start | bytes 319496 | tf_op jit(solution)/shard_map/ppermute | solution.py:138
  125.4 0.6 copy-start.10
  126.1 1.4 %copy-start.8 = (f32[416,32]{0,1:T(8,128)}, f32[416,32]{0,1:T(8,128)S(1)}, u32[]{:S(2)}) copy-start(f32[416,32]{0,1:T(8,128)S(1)} %slice.62) | copy-start | bytes 159748
  126.1 1.4 %copy-start.3 = (f32[192,416]{1,0:T(8,128)S(1)}, f32[192,416]{1,0:T(8,128)}, u32[]{:S(2)}) copy-start(f32[192,416]{1,0:T(8,128)} %param.12) | copy-start | bytes 958468
  126.1 1.4 %copy-start.4 = (f32[192,416]{1,0:T(8,128)S(1)}, f32[192,416]{1,0:T(8,128)}, u32[]{:S(2)}) copy-start(f32[192,416]{1,0:T(8,128)} %param.13) | copy-start | bytes 958468
